TPU v7x, 256 devices: a whole 4x4x8 slice. The times are simulated.
256 devices in a mesh: exp: 64 (over z, y, core), det: 4 (over x).
Axes of the slice: x: 4, y: 4, z: 8, core: 2. Of those that a mesh axis runs over, the one named last changes fastest.
Arguments:
- images: bfloat16 [2048, 8, 128, 128], P('exp', 'det'), may hold values from 0.5 to 2
- det_ids: int32 [2048, 8], P('exp', 'det'), may hold values from 0 to 7, each once within a row
- flat: float32 [8, 128, 128], P('det'), may hold values from 0.25 to 1.75
- backgrounds: float32 [2048, 8], P('exp', 'det'), may hold values from -3 to 3
- taps: bfloat16 [2048, 2, 15], P('exp'), may hold values from 0.019897461 to 0.25
- partner_dev: int32 [2048, 2], P('exp'), may hold values from 0 to 63, all different within a row; in each aligned block of 32 rows (0 to 31, 32 to 63, ...) at most 2 rows name the same one
- partner_slot: int32 [2048, 2], P('exp'), may hold values from 0 to 31
- offsets: int32 [2048, 2, 2], P('exp'), may hold values from -40 to 40
- pair_valid: int32 [2048, 2, 8], P('exp', None, 'det'), may hold values 0 or 1
Outputs:
- grad_flat: float32 [8, 128, 128], P('det', 'exp')
- grad_bkg: float32 [2048, 8], P('exp', 'det')
Inputs may be any that keep to these rules, and one draw needn't show every extreme that they name: `partner_dev`: among the 32 exposures of one device, no partner device is named by more than 2 of them, and each exposure names 2 different partner devices.
All inputs are finite; a program needn't handle non-finite values. No bound on the sum of `pair_valid` on one device may be relied on, other than what follows from the above.
Results may differ from a plain program's by a relative error of at most 0.0003.
Values may be sent and summed in bfloat16 or wider, within the bound.
No kernel may reach another device: no remote copies, remote signals or barrier semaphores. Data moves between devices by JAX's collectives and lax.ppermute only.
A program may use at most 128 MiB of HBM per device.

v0:
```python
import math

import jax
import jax.numpy as jnp
from jax import lax
from jax.sharding import PartitionSpec as P


def shift_mats(offs, pixels):
    rows = jnp.arange(pixels, dtype=jnp.int32)
    return (rows[None, None, :] == rows[None, :, None] + offs[:, None, None]).astype(jnp.bfloat16)


def apply_shift(field, row_mats, col_mats):
    partial_cols = jnp.einsum(
        "qduv,qxv->qdux", field, col_mats, preferred_element_type=jnp.float32
    ).astype(jnp.bfloat16)
    return jnp.einsum("qyu,qdux->qdyx", row_mats, partial_cols, preferred_element_type=jnp.float32)


def intersection_masks(row_offs, col_offs, pixels):
    rows = jnp.arange(pixels, dtype=jnp.int32)
    row_in = (rows[None, :] + row_offs[:, None] >= 0) & (rows[None, :] + row_offs[:, None] < pixels)
    col_in = (rows[None, :] + col_offs[:, None] >= 0) & (rows[None, :] + col_offs[:, None] < pixels)
    return (row_in[:, :, None] & col_in[:, None, :]).astype(jnp.float32)


def body(images, det_ids, flat, backgrounds, taps, partner_dev, partner_slot, offsets, pair_valid):
    high = lax.Precision.HIGHEST
    exp_dev, det_dev, pixels = (images.shape[0], images.shape[1], images.shape[2])
    pair_count = partner_dev.shape[1]
    tap_count = taps.shape[2]
    n_exp = lax.axis_size("exp")
    exp_here = lax.axis_index("exp")
    det_here = lax.axis_index("det")
    queries = exp_dev * pair_count
    all_flat = lax.all_gather(flat, "det", axis=0, tiled=True)
    det_total = all_flat.shape[0]
    pick = (det_ids[:, :, None] == jnp.arange(det_total, dtype=jnp.int32)[None, None, :]).astype(
        jnp.float32
    )
    gains = jnp.einsum("edg,gpq->edpq", pick, all_flat, precision=high)
    calibrated = (gains * images.astype(jnp.float32) - backgrounds[:, :, None, None]).astype(
        jnp.bfloat16
    )
    rows = jnp.arange(pixels, dtype=jnp.int32)
    lag = rows[None, :] - rows[:, None] + (tap_count - 1) // 2
    table = (lag[:, :, None] == jnp.arange(tap_count, dtype=jnp.int32)[None, None, :]).astype(
        jnp.bfloat16
    )
    bands = jnp.einsum("pqt,ekt->ekpq", table, taps, preferred_element_type=jnp.float32).astype(
        jnp.bfloat16
    )
    along_rows = bands[:, 0]
    along_cols = bands[:, 1]
    half_done = jnp.einsum(
        "edyw,exw->edyx", calibrated, along_cols, preferred_element_type=jnp.float32
    ).astype(jnp.bfloat16)
    psf_matched_images = jnp.einsum(
        "evy,edyx->edvx", along_rows, half_done, preferred_element_type=jnp.float32
    ).astype(jnp.bfloat16)
    dest = partner_dev.reshape(-1)
    wanted = partner_slot.reshape(-1)
    row_offs = offsets[:, :, 0].reshape(-1)
    col_offs = offsets[:, :, 1].reshape(-1)
    valid_flat = pair_valid.reshape(queries, det_dev)
    cap = max(2, 2 * exp_dev * pair_count // n_exp)
    slots_all = n_exp * cap
    hits = (dest[:, None] == jnp.arange(n_exp, dtype=jnp.int32)[None, :]).astype(jnp.int32)
    before = jnp.cumsum(hits, axis=0) - hits
    rank = jnp.sum(before * hits, axis=1)
    slot = dest * cap + rank
    placement_table = (slot[None, :] == jnp.arange(slots_all, dtype=jnp.int32)[:, None]).astype(
        jnp.bfloat16
    )
    out_ids = jnp.zeros((slots_all,), jnp.int32).at[slot].set(wanted + 1).reshape(n_exp, cap)
    outgoing_shift = (
        jnp.zeros((slots_all, 2), jnp.int32)
        .at[slot]
        .set(offsets.reshape(queries, 2))
        .reshape(n_exp, cap, 2)
    )
    out_valid = (
        jnp.zeros((slots_all, det_dev), jnp.int32)
        .at[slot]
        .set(valid_flat)
        .reshape(n_exp, cap, det_dev)
    )
    in_ids, in_shift, in_valid = (
        lax.all_to_all(out_ids, "exp", split_axis=0, concat_axis=0, tiled=True),
        lax.all_to_all(outgoing_shift, "exp", split_axis=0, concat_axis=0, tiled=True),
        lax.all_to_all(out_valid, "exp", split_axis=0, concat_axis=0, tiled=True),
    )
    incoming = in_ids.reshape(-1)
    in_shift = in_shift.reshape(slots_all, 2)
    in_valid = in_valid.reshape(slots_all, det_dev)
    served_selection = (
        incoming[:, None] - 1 == jnp.arange(exp_dev, dtype=jnp.int32)[None, :]
    ).astype(jnp.bfloat16)
    served_flat = jnp.einsum(
        "lm,muqo->luqo", served_selection, psf_matched_images, preferred_element_type=jnp.float32
    ).astype(jnp.bfloat16)
    served = served_flat.reshape(n_exp, cap, det_dev, pixels, pixels)
    returned = lax.all_to_all(served, "exp", split_axis=0, concat_axis=0, tiled=True)
    partners = jnp.einsum(
        "fj,fvhm->jvhm",
        placement_table,
        returned.reshape(slots_all, det_dev, pixels, pixels),
        preferred_element_type=jnp.float32,
    ).astype(jnp.bfloat16)
    moved = apply_shift(partners, shift_mats(row_offs, pixels), shift_mats(col_offs, pixels))
    intersection = intersection_masks(row_offs, col_offs, pixels).reshape(
        exp_dev, pair_count, 1, pixels, pixels
    )
    weight = pair_valid.astype(jnp.float32).reshape(exp_dev, pair_count, det_dev, 1, 1)
    moved = moved.reshape(exp_dev, pair_count, det_dev, pixels, pixels)
    resid = weight * intersection * (psf_matched_images[:, None].astype(jnp.float32) - moved)
    adj_own = jnp.sum(resid, axis=1)
    resid_low = resid.reshape(queries, det_dev, pixels, pixels).astype(jnp.bfloat16)
    returned_images = apply_shift(
        resid_low, shift_mats(-row_offs, pixels), shift_mats(-col_offs, pixels)
    ).astype(jnp.bfloat16)
    sending_images = jnp.einsum(
        "ea,ajhv->ejhv", placement_table, returned_images, preferred_element_type=jnp.float32
    ).astype(jnp.bfloat16)
    sending_images = sending_images.reshape(n_exp, cap, det_dev, pixels, pixels)
    arrived = lax.all_to_all(
        sending_images, "exp", split_axis=0, concat_axis=0, tiled=True
    ).reshape(slots_all, det_dev, pixels, pixels)
    owners = (incoming[None, :] - 1 == jnp.arange(exp_dev, dtype=jnp.int32)[:, None]).astype(
        jnp.bfloat16
    )
    adj_partner = jnp.einsum("js,sdpq->jdpq", owners, arrived, preferred_element_type=jnp.float32)
    adj_matched = adj_own - adj_partner
    partial_rows = jnp.einsum(
        "edyx,exw->edyw", adj_matched, along_cols.astype(jnp.float32), precision=high
    )
    adj_cal = jnp.einsum(
        "eyv,edyw->edvw", along_rows.astype(jnp.float32), partial_rows, precision=high
    )
    grad_bkg = -jnp.sum(adj_cal, axis=(2, 3)) / pixels
    flat_norm = 1.0 / math.sqrt(2.0 * pair_count * exp_dev * n_exp)
    terms = jnp.einsum(
        "edg,edpq->gpq", pick, images.astype(jnp.float32) * adj_cal * flat_norm, precision=high
    )
    band_rows = pixels // n_exp
    summed = lax.psum(terms, ("exp", "det"))
    grad_flat = lax.dynamic_slice(
        summed,
        (det_here * det_dev, exp_here * band_rows, jnp.int32(0)),
        (det_dev, band_rows, pixels),
    )
    return (grad_flat, grad_bkg)


def solution(mesh):
    return jax.shard_map(
        body,
        mesh=mesh,
        in_specs=(
            P("exp", "det", None, None),
            P("exp", "det"),
            P("det", None, None),
            P("exp", "det"),
            P("exp", None, None),
            P("exp", None),
            P("exp", None),
            P("exp", None, None),
            P("exp", None, "det"),
        ),
        out_specs=(P("det", "exp", None), P("exp", "det")),
        check_vma=False,
    )
```

profile of v0, /device:TPU:1, one launch (start us, length us, event | category | flops | bytes accessed | tf_op | source)
XLA Modules:
  0.0 819.1 jit_solution(15353940844444523913)
XLA Ops:
  11.8 13.1 %all-to-all-start = ((s32[64,1,2]{2,1,0:T(1,128)}), s32[64,1,2]{2,1,0:T(1,128)S(1)}, u32[]{:S(2)}, u32[]{:S(2)}) async-start(s32[64,1,2]{2,1,0:T(1,128)} %bitcast.18), calls=%async_computation | async-start | bytes 65536 | tf_op jit(solution)/shard_map/all_to_all | solution.py:90
  27.0 11.1 %all_gather.3 = f32[8,128,128]{2,1,0:T(8,128)S(1)} all-gather(f32[2,128,128]{2,1,0:T(8,128)S(1)} %copy-done.3), channel_id=1, replica_groups=mesh['exp'=64,'det'=4] {'det'}, dimensions={0}, use_global_device_ids=true | all-gather | bytes 655360 | tf_op jit(solution)/shard_map/all_gather | solution.py:37
  38.0 7.6 fusion.3
  45.7 6.1 fusion.101
  51.8 4.6 copy.61
  60.5 7.0 copy.62
  67.6 21.5 %all-to-all-start.1 = ((bf16[64,2,2,128,128]{4,1,3,2,0:T(2,128)(2,1)}), bf16[64,2,2,128,128]{4,1,3,2,0:T(2,128)(2,1)}, u32[]{:S(2)}, u32[]{:S(2)}) async-start(bf16[64,2,2,128,128]{4,1,3,2,0:T(2,128)(2,1)} %copy.62), calls=%async_computation.1 | async-start | bytes 16777216 | tf_op jit(solution)/shard_map/all_to_all | solution.py:104
  96.4 175.7 %all-to-all-done.1 = bf16[64,2,2,128,128]{4,1,3,2,0:T(2,128)(2,1)} async-done(((bf16[64,2,2,128,128]{4,1,3,2,0:T(2,128)(2,1)}), bf16[64,2,2,128,128]{4,1,3,2,0:T(2,128)(2,1)}, u32[]{:S(2)}, u32[]{:S(2)}) %all-to-all-start.1) | async-done | bytes 8388640 | tf_op jit(solution)/shard_map/all_to_all | solution.py:104
  272.1 9.2 %copy.63 = bf16[64,2,2,128,128]{4,1,0,3,2:T(2,128)(2,1)S(1)} copy(bf16[64,2,2,128,128]{4,1,3,2,0:T(2,128)(2,1)} %all-to-all-done.1) | data formatting | bytes 16777216 | tf_op jit(solution)/shard_map/all_to_all | solution.py:104
  284.6 13.0 %multiply_reduce_fusion = (f32[32,2,128,128]{2,3,1,0:T(8,128)}, f32[64,2,128,128]{3,2,1,0:T(8,128)}) fusion(f32[32,2,128,128]{2,3,1,0:T(8,128)} %get-tuple-element.12, f32[32,2,128,128]{2,3,1,0:T(8,128)} %and_convert_fusion.1, f32[32,2,2]{2,1,0:T(2,128)S(1)} %copy.48, s32[64,128]{1,0:T(8,128)S(1)} %get-tuple-element.20, ...), kind=kOutput, calls=%fused_computation.4 | convolution fusion | flops 1085276160 | bytes 25231872 | tf_op jit(solution)/shard_map/qyu,qdux->qdyx/dot_general | solution.py:18
  297.6 8.6 %fusion.1 = bf16[64,2,128,128]{2,3,1,0:T(8,128)(2,1)} fusion(f32[64,2,128,128]{3,2,1,0:T(8,128)} %get-tuple-element.15, f32[64,128,128]{1,2,0:T(8,128)} %and_convert_fusion, f32[64,2]{1,0:T(8,128)S(1)} %bitcast.140, f32[32,2,128,128]{2,3,1,0:T(8,128)} %get-tuple-element.12), kind=kLoop, calls=%fused_computation.3 | loop fusion | flops 8388608 | bytes 20972032 | tf_op jit(solution)/shard_map/convert_element_type | solution.py:119
  306.2 8.1 convert_bitcast_fusion
  314.3 6.6 copy.72
  320.9 4.6 convolution_convert_fusion
  325.5 7.0 copy.73
  332.6 9.4 %all-to-all-start.2 = ((bf16[64,2,2,128,128]{4,1,3,2,0:T(2,128)(2,1)}), bf16[64,2,2,128,128]{4,1,3,2,0:T(2,128)(2,1)}, u32[]{:S(2)}, u32[]{:S(2)}) async-start(bf16[64,2,2,128,128]{4,1,3,2,0:T(2,128)(2,1)} %copy.73), calls=%async_computation.2 | async-start | bytes 16777216 | tf_op jit(solution)/shard_map/all_to_all | solution.py:127
  342.2 5.5 copy.75
  347.7 176.5 %all-to-all-done.2 = bf16[64,2,2,128,128]{4,1,3,2,0:T(2,128)(2,1)} async-done(((bf16[64,2,2,128,128]{4,1,3,2,0:T(2,128)(2,1)}), bf16[64,2,2,128,128]{4,1,3,2,0:T(2,128)(2,1)}, u32[]{:S(2)}, u32[]{:S(2)}) %all-to-all-start.2) | async-done | bytes 8388640 | tf_op jit(solution)/shard_map/all_to_all | solution.py:127
  524.3 9.4 %copy.74 = bf16[64,2,2,128,128]{4,1,0,3,2:T(2,128)(2,1)S(1)} copy(bf16[64,2,2,128,128]{4,1,3,2,0:T(2,128)(2,1)} %all-to-all-done.2) | data formatting | bytes 16777216 | tf_op jit(solution)/shard_map/all_to_all | solution.py:127
  534.9 5.2 fusion.8
  540.1 4.4 bitcast_reduce_fusion
  544.5 5.7 copy.80
  550.2 5.7 fusion.63
  556.6 254.0 %all-reduce.2.cloned.1.call-done = f32[8,128,128]{2,0,1:T(8,128)} async-done(((f32[8,128,128]{2,0,1:T(8,128)}), f32[8,128,128]{2,0,1:T(8,128)}) %all-reduce.2.cloned.1.call-update) | async-done | bytes 524304 | tf_op jit(solution)/shard_map/psum | solution.py:147
  (63 shorter events, 24.6 us)
Async XLA Ops:
  7.2 19.8 %copy-start.3 = (f32[2,128,128]{2,1,0:T(8,128)S(1)}, f32[2,128,128]{2,1,0:T(8,128)}, u32[]{:S(2)}) copy-start(f32[2,128,128]{2,1,0:T(8,128)} %param.11) | copy-start | bytes 393220
  7.2 30.8 %copy-start.4 = (s32[32,2]{0,1:T(2,128)S(1)}, s32[32,2]{0,1:T(2,128)}, u32[]{:S(2)}) copy-start(s32[32,2]{0,1:T(2,128)} %param.10) | copy-start | bytes 772
  7.2 30.8 %copy-start.7 = (f32[32,2]{0,1:T(2,128)S(1)}, f32[32,2]{0,1:T(2,128)}, u32[]{:S(2)}) copy-start(f32[32,2]{0,1:T(2,128)} %param.12) | copy-start | bytes 772
  11.8 44.5 %all-to-all-start = ((s32[64,1,2]{2,1,0:T(1,128)}), s32[64,1,2]{2,1,0:T(1,128)S(1)}, u32[]{:S(2)}, u32[]{:S(2)}) async-start(s32[64,1,2]{2,1,0:T(1,128)} %bitcast.18), calls=%async_computation | async-start | bytes 65536 | tf_op jit(solution)/shard_map/all_to_all | solution.py:90
  24.9 13.1 %copy-start.1 = (bf16[32,2,128,128]{3,2,1,0:T(8,128)(2,1)S(1)}, bf16[32,2,128,128]{3,2,1,0:T(8,128)(2,1)}, u32[]{:S(2)}) copy-start(bf16[32,2,128,128]{3,2,1,0:T(8,128)(2,1)} %param.9) | copy-start | bytes 6291460
  67.6 21.5 %copy-start.5 = (s32[32,2,2]{0,2,1:T(2,128)S(1)}, s32[32,2,2]{0,2,1:T(2,128)}, u32[]{:S(2)}) copy-start(s32[32,2,2]{0,2,1:T(2,128)} %param.16) | copy-start | bytes 1540
  67.6 22.1 %copy-start.6 = (s32[32,2,2]{0,2,1:T(2,128)S(1)}, s32[32,2,2]{0,2,1:T(2,128)}, u32[]{:S(2)}) copy-start(s32[32,2,2]{0,2,1:T(2,128)} %param.17) | copy-start | bytes 1540
  67.6 204.5 %all-to-all-start.1 = ((bf16[64,2,2,128,128]{4,1,3,2,0:T(2,128)(2,1)}), bf16[64,2,2,128,128]{4,1,3,2,0:T(2,128)(2,1)}, u32[]{:S(2)}, u32[]{:S(2)}) async-start(bf16[64,2,2,128,128]{4,1,3,2,0:T(2,128)(2,1)} %copy.62), calls=%async_computation.1 | async-start | bytes 16777216 | tf_op jit(solution)/shard_map/all_to_all | solution.py:104
  332.6 191.7 %all-to-all-start.2 = ((bf16[64,2,2,128,128]{4,1,3,2,0:T(2,128)(2,1)}), bf16[64,2,2,128,128]{4,1,3,2,0:T(2,128)(2,1)}, u32[]{:S(2)}, u32[]{:S(2)}) async-start(bf16[64,2,2,128,128]{4,1,3,2,0:T(2,128)(2,1)} %copy.73), calls=%async_computation.2 | async-start | bytes 16777216 | tf_op jit(solution)/shard_map/all_to_all | solution.py:127
  342.0 468.6 %all-reduce.2.cloned.1.call-start = ((), (), s32[]{:S(2)}) async-start(), calls=%async_computation.3 | async-start | bytes 1048576 | tf_op jit(solution)/shard_map/psum | solution.py:147
  524.3 9.4 %copy-start = (f32[32,2,128,128]{3,0,2,1:T(8,128)S(1)}, f32[32,2,128,128]{3,0,2,1:T(8,128)}, u32[]{:S(2)}) copy-start(f32[32,2,128,128]{3,0,2,1:T(8,128)} %copy.75) | copy-start | bytes 12582916
  544.5 5.7 copy-start.2
Sparse Core Ops, SparseCore 0:
  556.0 254.5 all-reduce.1
where the time goes:
time: 830 us; the launch traced here: 819 us
  waiting for transfers between devices  606 us (73%)
  matrix products  64.9 us (8%)
  local copies, waits for them, and re-layouts  60.9 us (7%)
  starting transfers between devices  44.3 us (5%)
  other arithmetic  17 us (2%)
  between operations  14.7 us (2%)
  blocking collectives  11.1 us (1%)
    psum x1, waiting for transfers between devices, body(): summed = lax.psum(terms, ('exp', 'det'))  254 us
    all_to_all x1, waiting for transfers between devices, body(): lax.all_to_all(sending_images, 'exp', split_axis=0, concat_axis=0, tiled=...  177 us
    all_to_all x1, waiting for transfers between devices, body(): lax.all_to_all(served, 'exp', split_axis=0, concat_axis=0, tiled=True)  176 us
    all_to_all x1, starting transfers between devices, body(): lax.all_to_all(served, 'exp', split_axis=0, concat_axis=0, tiled=True)  21.5 us
    dot_general x2, matrix products, apply_shift(): jnp.einsum('qyu,qdux->qdyx', row_mats, partial_cols, preferred_element_ty...  21.1 us
  transfers between devices with their start and end apart: 4, of which 3 were waited for; matrix products, arithmetic and copies ran while one was open for 4% of the time, Pallas kernels for 0%

commit v1 on v0

--- a/solution.py
+++ b/solution.py
@@ -143,12 +143,11 @@
     terms = jnp.einsum(
         "edg,edpq->gpq", pick, images.astype(jnp.float32) * adj_cal * flat_norm, precision=high
     )
+    by_det = lax.psum_scatter(terms, "det", scatter_dimension=0, tiled=True)
     band_rows = pixels // n_exp
-    summed = lax.psum(terms, ("exp", "det"))
-    grad_flat = lax.dynamic_slice(
-        summed,
-        (det_here * det_dev, exp_here * band_rows, jnp.int32(0)),
-        (det_dev, band_rows, pixels),
+    by_band = by_det.reshape(det_dev, n_exp, band_rows, pixels).transpose(1, 0, 2, 3)
+    grad_flat = jnp.sum(
+        lax.all_to_all(by_band, "exp", split_axis=0, concat_axis=0, tiled=True), axis=0
     )
     return (grad_flat, grad_bkg)
 

time: 830 us -> 613 us (0.74)
  waiting for transfers between devices: 606 us -> 385 us
    psum x1 -> x0, waiting for transfers between devices: 254 us -> none  [body(): summed = lax.psum(terms, ('exp', 'det'))]
    reduce_scatter x0 -> x1, waiting for transfers between devices: none -> 22.7 us  [body(): by_det = lax.psum_scatter(terms, 'det', scatter_dimension=0, tiled=True)]
    all_to_all x0 -> x1, starting transfers between devices: none -> 13.1 us  [body(): lax.all_to_all(by_band, 'exp', split_axis=0, concat_axis=0, tiled=True)]
    all_to_all x0 -> x1, waiting for transfers between devices: none -> 10.4 us  [body(): lax.all_to_all(by_band, 'exp', split_axis=0, concat_axis=0, tiled=True)]
    all_to_all x1, starting transfers between devices: 21.5 us -> 12.9 us  [body(): lax.all_to_all(served, 'exp', split_axis=0, concat_axis=0, tiled=True)]
  transfers between devices with their start and end apart: 4 -> 5, of which waited for: 3 -> 4; matrix products, arithmetic and copies ran while one was open for 4% -> 6% of each run, Pallas kernels for 0% -> 0%
where the time goes in v1:
time: 613 us; the launch traced here: 604 us
  waiting for transfers between devices  385 us (63%)
  matrix products  64 us (10%)
  local copies, waits for them, and re-layouts  63 us (10%)
  starting transfers between devices  49.4 us (8%)
  other arithmetic  17 us (3%)
  between operations  14.8 us (2%)
  blocking collectives  11.1 us (2%)
    all_to_all x1, waiting for transfers between devices, body(): lax.all_to_all(sending_images, 'exp', split_axis=0, concat_axis=0, tiled=...  177 us
    all_to_all x1, waiting for transfers between devices, body(): lax.all_to_all(served, 'exp', split_axis=0, concat_axis=0, tiled=True)  175 us
    reduce_scatter x1, waiting for transfers between devices, body(): by_det = lax.psum_scatter(terms, 'det', scatter_dimension=0, tiled=True)  22.7 us
    dot_general x2, matrix products, apply_shift(): jnp.einsum('qyu,qdux->qdyx', row_mats, partial_cols, preferred_element_ty...  21.1 us
    all_to_all x1, starting transfers between devices, body(): lax.all_to_all(out_ids, 'exp', split_axis=0, concat_axis=0, tiled=True)  13.1 us
    all_to_all x1, starting transfers between devices, body(): lax.all_to_all(by_band, 'exp', split_axis=0, concat_axis=0, tiled=True)  13.1 us
    all_to_all x1, starting transfers between devices, body(): lax.all_to_all(served, 'exp', split_axis=0, concat_axis=0, tiled=True)  12.9 us
  transfers between devices with their start and end apart: 5, of which 4 were waited for; matrix products, arithmetic and copies ran while one was open for 6% of the time, Pallas kernels for 0%

profile of v1, /device:TPU:1, one launch (start us, length us, event | category | flops | bytes accessed | tf_op | source)
XLA Modules:
  0.0 604.2 jit_solution(3051031826450678852)
XLA Ops:
  11.8 13.1 %all-to-all-start = ((s32[64,1,2]{2,1,0:T(1,128)}), s32[64,1,2]{2,1,0:T(1,128)S(1)}, u32[]{:S(2)}, u32[]{:S(2)}) async-start(s32[64,1,2]{2,1,0:T(1,128)} %bitcast.18), calls=%async_computation | async-start | bytes 65536 | tf_op jit(solution)/shard_map/all_to_all | solution.py:90
  26.9 11.1 %all_gather.3 = f32[8,128,128]{2,1,0:T(8,128)S(1)} all-gather(f32[2,128,128]{2,1,0:T(8,128)S(1)} %copy-done.3), channel_id=1, replica_groups=mesh['exp'=64,'det'=4] {'det'}, dimensions={0}, use_global_device_ids=true | all-gather | bytes 655360 | tf_op jit(solution)/shard_map/all_gather | solution.py:37
  38.0 7.7 %fusion.3 = bf16[32,2,128,128]{3,0,2,1:T(8,128)(2,1)} fusion(f32[32,2]{0,1:T(2,128)S(1)} %copy-done.7, bf16[32,2,128,128]{3,2,1,0:T(8,128)(2,1)S(1)} %copy-done.1, f32[8,128,128]{2,1,0:T(8,128)S(1)} %all_gather.3, s32[32,2]{0,1:T(2,128)S(1)} %copy-done.4), kind=kOutput, calls=%fused_computation.10 | convolution fusion | flops 104858112 | bytes 4719104 | tf_op jit(solution)/shard_map/edg,gpq->edpq/dot_general | solution.py:42
  45.7 6.1 %fusion.101 = (f32[32,2,128,128]{2,3,1,0:T(8,128)}, bf16[32,2,128,128]{2,3,1,0:T(8,128)(2,1)}) fusion(bf16[32,128,128,1]{2,0,1,3:T(8,128)(2,1)S(1)} %get-tuple-element.5, bf16[32,2,128,128]{3,0,2,1:T(8,128)(2,1)} %fusion.3, bf16[32,128,128,1]{2,0,1,3:T(8,128)(2,1)S(1)} %get-tuple-element.4), kind=kOutput, calls=%fused_computation.103 | convolution fusion | flops 540016640 | bytes 10485760 | tf_op jit(solution)/shard_map/evy,edyx->edvx/dot_general | solution.py:59
  60.5 7.0 %copy.60 = bf16[64,2,2,128,128]{4,1,3,2,0:T(2,128)(2,1)} copy(bf16[64,2,2,128,128]{4,1,0,3,2:T(2,128)(2,1)S(1)} %bitcast.142) | data formatting | bytes 16777216 | tf_op jit(solution)/shard_map/reshape | solution.py:103
  67.5 12.9 %all-to-all-start.1 = ((bf16[64,2,2,128,128]{4,1,3,2,0:T(2,128)(2,1)}), bf16[64,2,2,128,128]{4,1,3,2,0:T(2,128)(2,1)}, u32[]{:S(2)}, u32[]{:S(2)}) async-start(bf16[64,2,2,128,128]{4,1,3,2,0:T(2,128)(2,1)} %copy.60), calls=%async_computation.1 | async-start | bytes 16777216 | tf_op jit(solution)/shard_map/all_to_all | solution.py:104
  87.7 175.0 %all-to-all-done.1 = bf16[64,2,2,128,128]{4,1,3,2,0:T(2,128)(2,1)} async-done(((bf16[64,2,2,128,128]{4,1,3,2,0:T(2,128)(2,1)}), bf16[64,2,2,128,128]{4,1,3,2,0:T(2,128)(2,1)}, u32[]{:S(2)}, u32[]{:S(2)}) %all-to-all-start.1) | async-done | bytes 8388640 | tf_op jit(solution)/shard_map/all_to_all | solution.py:104
  262.7 9.2 %copy.61 = bf16[64,2,2,128,128]{4,1,0,3,2:T(2,128)(2,1)S(1)} copy(bf16[64,2,2,128,128]{4,1,3,2,0:T(2,128)(2,1)} %all-to-all-done.1) | data formatting | bytes 16777216 | tf_op jit(solution)/shard_map/all_to_all | solution.py:104
  275.2 13.0 %multiply_reduce_fusion = (f32[32,2,128,128]{2,3,1,0:T(8,128)}, f32[64,2,128,128]{3,2,1,0:T(8,128)}) fusion(f32[32,2,128,128]{2,3,1,0:T(8,128)} %get-tuple-element.8, f32[32,2,128,128]{2,3,1,0:T(8,128)} %and_convert_fusion.1, f32[32,2,2]{2,1,0:T(2,128)S(1)} %copy.46, s32[64,128]{1,0:T(8,128)S(1)} %get-tuple-element.16, ...), kind=kOutput, calls=%fused_computation.4 | convolution fusion | flops 1085276160 | bytes 25231872 | tf_op jit(solution)/shard_map/qyu,qdux->qdyx/dot_general | solution.py:18
  288.3 8.6 %fusion.1 = bf16[64,2,128,128]{2,3,1,0:T(8,128)(2,1)} fusion(f32[64,2,128,128]{3,2,1,0:T(8,128)} %get-tuple-element.11, f32[64,128,128]{1,2,0:T(8,128)} %and_convert_fusion, f32[64,2]{1,0:T(8,128)S(1)} %bitcast.144, f32[32,2,128,128]{2,3,1,0:T(8,128)} %get-tuple-element.8), kind=kLoop, calls=%fused_computation.3 | loop fusion | flops 8388608 | bytes 20972032 | tf_op jit(solution)/shard_map/convert_element_type | solution.py:119
  296.9 8.1 %convert_bitcast_fusion = bf16[64,2,128,128]{2,3,1,0:T(8,128)(2,1)} fusion(bf16[64,2,128,128]{2,3,1,0:T(8,128)(2,1)} %fusion.1, s32[64,128]{1,0:T(8,128)S(1)} %get-tuple-element.20, s32[64,128]{1,0:T(8,128)S(1)} %get-tuple-element.21), kind=kOutput, calls=%fused_computation.19 | convolution fusion | flops 1080033280 | bytes 8454144 | tf_op jit(solution)/shard_map/qyu,qdux->qdyx/dot_general | solution.py:18
  304.9 6.6 %copy.70 = bf16[64,2,128,128]{3,0,2,1:T(8,128)(2,1)} copy(bf16[64,2,128,128]{2,3,1,0:T(8,128)(2,1)} %convert_bitcast_fusion) | data formatting | bytes 8388608 | tf_op jit(solution)/shard_map/convert_element_type | solution.py:122
  311.5 4.6 convolution_convert_fusion
  316.1 7.0 %copy.71 = bf16[64,2,2,128,128]{4,1,3,2,0:T(2,128)(2,1)} copy(bf16[64,2,2,128,128]{4,1,0,3,2:T(2,128)(2,1)S(1)} %bitcast.141) | data formatting | bytes 16777216 | tf_op jit(solution)/shard_map/reshape | solution.py:126
  323.1 10.3 %all-to-all-start.2 = ((bf16[64,2,2,128,128]{4,1,3,2,0:T(2,128)(2,1)}), bf16[64,2,2,128,128]{4,1,3,2,0:T(2,128)(2,1)}, u32[]{:S(2)}, u32[]{:S(2)}) async-start(bf16[64,2,2,128,128]{4,1,3,2,0:T(2,128)(2,1)} %copy.71), calls=%async_computation.2 | async-start | bytes 16777216 | tf_op jit(solution)/shard_map/all_to_all | solution.py:127
  333.5 5.5 copy.73
  339.0 176.7 %all-to-all-done.2 = bf16[64,2,2,128,128]{4,1,3,2,0:T(2,128)(2,1)} async-done(((bf16[64,2,2,128,128]{4,1,3,2,0:T(2,128)(2,1)}), bf16[64,2,2,128,128]{4,1,3,2,0:T(2,128)(2,1)}, u32[]{:S(2)}, u32[]{:S(2)}) %all-to-all-start.2) | async-done | bytes 8388640 | tf_op jit(solution)/shard_map/all_to_all | solution.py:127
  515.7 9.4 %copy.72 = bf16[64,2,2,128,128]{4,1,0,3,2:T(2,128)(2,1)S(1)} copy(bf16[64,2,2,128,128]{4,1,3,2,0:T(2,128)(2,1)} %all-to-all-done.2) | data formatting | bytes 16777216 | tf_op jit(solution)/shard_map/all_to_all | solution.py:127
  526.4 5.2 fusion.8
  535.9 5.9 copy.78
  541.8 4.9 fusion.63
  547.7 22.7 %reduce-scatter.2.cloned.1.call-done = f32[2,128,128]{2,1,0:T(8,128)} async-done(((f32[8,128,128]{2,1,0:T(8,128)}), f32[2,128,128]{2,1,0:T(8,128)}) %reduce-scatter.2.cloned.1.call-update) | async-done | bytes 131088 | tf_op jit(solution)/shard_map/reduce_scatter | solution.py:146
  572.0 13.1 %all-to-all-start.3 = ((f32[64,2,2,128]{3,1,2,0:T(2,128)}), f32[64,2,2,128]{3,1,2,0:T(2,128)S(1)}, u32[]{:S(2)}, u32[]{:S(2)}) async-start(f32[64,2,2,128]{3,1,2,0:T(2,128)} %bitcast.139), calls=%async_computation.4 | async-start | bytes 262144 | tf_op jit(solution)/shard_map/all_to_all | solution.py:150
  585.8 10.4 %all-to-all-done.3 = f32[64,2,2,128]{3,1,2,0:T(2,128)S(1)} async-done(((f32[64,2,2,128]{3,1,2,0:T(2,128)}), f32[64,2,2,128]{3,1,2,0:T(2,128)S(1)}, u32[]{:S(2)}, u32[]{:S(2)}) %all-to-all-start.3) | async-done | bytes 131104 | tf_op jit(solution)/shard_map/all_to_all | solution.py:150
  (67 shorter events, 35.2 us)
Async XLA Ops:
  7.2 19.8 %copy-start.3 = (f32[2,128,128]{2,1,0:T(8,128)S(1)}, f32[2,128,128]{2,1,0:T(8,128)}, u32[]{:S(2)}) copy-start(f32[2,128,128]{2,1,0:T(8,128)} %param.11) | copy-start | bytes 393220
  7.2 30.8 %copy-start.4 = (s32[32,2]{0,1:T(2,128)S(1)}, s32[32,2]{0,1:T(2,128)}, u32[]{:S(2)}) copy-start(s32[32,2]{0,1:T(2,128)} %param.10) | copy-start | bytes 772
  7.2 30.8 %copy-start.7 = (f32[32,2]{0,1:T(2,128)S(1)}, f32[32,2]{0,1:T(2,128)}, u32[]{:S(2)}) copy-start(f32[32,2]{0,1:T(2,128)} %param.12) | copy-start | bytes 772
  11.8 44.5 %all-to-all-start = ((s32[64,1,2]{2,1,0:T(1,128)}), s32[64,1,2]{2,1,0:T(1,128)S(1)}, u32[]{:S(2)}, u32[]{:S(2)}) async-start(s32[64,1,2]{2,1,0:T(1,128)} %bitcast.18), calls=%async_computation | async-start | bytes 65536 | tf_op jit(solution)/shard_map/all_to_all | solution.py:90
  24.9 13.1 %copy-start.1 = (bf16[32,2,128,128]{3,2,1,0:T(8,128)(2,1)S(1)}, bf16[32,2,128,128]{3,2,1,0:T(8,128)(2,1)}, u32[]{:S(2)}) copy-start(bf16[32,2,128,128]{3,2,1,0:T(8,128)(2,1)} %param.9) | copy-start | bytes 6291460
  67.5 12.9 %copy-start.5 = (s32[32,2,2]{0,2,1:T(2,128)S(1)}, s32[32,2,2]{0,2,1:T(2,128)}, u32[]{:S(2)}) copy-start(s32[32,2,2]{0,2,1:T(2,128)} %param.16) | copy-start | bytes 1540
  67.5 13.5 %copy-start.6 = (s32[32,2,2]{0,2,1:T(2,128)S(1)}, s32[32,2,2]{0,2,1:T(2,128)}, u32[]{:S(2)}) copy-start(s32[32,2,2]{0,2,1:T(2,128)} %param.17) | copy-start | bytes 1540
  67.5 195.2 %all-to-all-start.1 = ((bf16[64,2,2,128,128]{4,1,3,2,0:T(2,128)(2,1)}), bf16[64,2,2,128,128]{4,1,3,2,0:T(2,128)(2,1)}, u32[]{:S(2)}, u32[]{:S(2)}) async-start(bf16[64,2,2,128,128]{4,1,3,2,0:T(2,128)(2,1)} %copy.60), calls=%async_computation.1 | async-start | bytes 16777216 | tf_op jit(solution)/shard_map/all_to_all | solution.py:104
  323.1 192.6 %all-to-all-start.2 = ((bf16[64,2,2,128,128]{4,1,3,2,0:T(2,128)(2,1)}), bf16[64,2,2,128,128]{4,1,3,2,0:T(2,128)(2,1)}, u32[]{:S(2)}, u32[]{:S(2)}) async-start(bf16[64,2,2,128,128]{4,1,3,2,0:T(2,128)(2,1)} %copy.71), calls=%async_computation.2 | async-start | bytes 16777216 | tf_op jit(solution)/shard_map/all_to_all | solution.py:127
  333.4 237.0 %reduce-scatter.2.cloned.1.call-start = ((), (), s32[]{:S(2)}) async-start(), calls=%async_computation.5 | async-start | bytes 655360 | tf_op jit(solution)/shard_map/reduce_scatter | solution.py:146
  515.7 9.4 %copy-start = (f32[32,2,128,128]{3,0,2,1:T(8,128)S(1)}, f32[32,2,128,128]{3,0,2,1:T(8,128)}, u32[]{:S(2)}) copy-start(f32[32,2,128,128]{3,0,2,1:T(8,128)} %copy.73) | copy-start | bytes 12582916
  535.9 5.9 copy-start.2
  572.0 24.2 %all-to-all-start.3 = ((f32[64,2,2,128]{3,1,2,0:T(2,128)}), f32[64,2,2,128]{3,1,2,0:T(2,128)S(1)}, u32[]{:S(2)}, u32[]{:S(2)}) async-start(f32[64,2,2,128]{3,1,2,0:T(2,128)} %bitcast.139), calls=%async_computation.4 | async-start | bytes 262144 | tf_op jit(solution)/shard_map/all_to_all | solution.py:150
Sparse Core Ops, SparseCore 0:
  547.8 22.5 reduce-scatter.1

commit v2 on v1

v2 whole, which is shorter than its diff:
```python
import math

import jax
import jax.numpy as jnp
from jax import lax
from jax.sharding import PartitionSpec as P


def shift_mats(offs, pixels):
    rows = jnp.arange(pixels, dtype=jnp.int32)
    return (rows[None, None, :] == rows[None, :, None] + offs[:, None, None]).astype(jnp.bfloat16)


def apply_shift(field, row_mats, col_mats):
    partial_cols = jnp.einsum(
        "qduv,qxv->qdux", field, col_mats, preferred_element_type=jnp.float32
    ).astype(jnp.bfloat16)
    return jnp.einsum("qyu,qdux->qdyx", row_mats, partial_cols, preferred_element_type=jnp.float32)


def intersection_masks(row_offs, col_offs, pixels):
    rows = jnp.arange(pixels, dtype=jnp.int32)
    row_in = (rows[None, :] + row_offs[:, None] >= 0) & (rows[None, :] + row_offs[:, None] < pixels)
    col_in = (rows[None, :] + col_offs[:, None] >= 0) & (rows[None, :] + col_offs[:, None] < pixels)
    return (row_in[:, :, None] & col_in[:, None, :]).astype(jnp.float32)


def body(images, det_ids, flat, backgrounds, taps, partner_dev, partner_slot, offsets, pair_valid):
    high = lax.Precision.HIGHEST
    exp_dev, det_dev, pixels = (images.shape[0], images.shape[1], images.shape[2])
    pair_count = partner_dev.shape[1]
    tap_count = taps.shape[2]
    n_exp = lax.axis_size("exp")
    queries = exp_dev * pair_count
    all_flat = lax.all_gather(flat, "det", axis=0, tiled=True)
    det_total = all_flat.shape[0]
    pick = (det_ids[:, :, None] == jnp.arange(det_total, dtype=jnp.int32)[None, None, :]).astype(
        jnp.float32
    )
    rows = jnp.arange(pixels, dtype=jnp.int32)
    lag = rows[None, :] - rows[:, None] + (tap_count - 1) // 2
    table = (lag[:, :, None] == jnp.arange(tap_count, dtype=jnp.int32)[None, None, :]).astype(
        jnp.bfloat16
    )
    bands = jnp.einsum("pqt,ekt->ekpq", table, taps, preferred_element_type=jnp.float32).astype(
        jnp.bfloat16
    )
    along_rows = bands[:, 0]
    along_cols = bands[:, 1]
    dest = partner_dev.reshape(-1)
    wanted = partner_slot.reshape(-1)
    row_offs = offsets[:, :, 0].reshape(-1)
    col_offs = offsets[:, :, 1].reshape(-1)
    valid_flat = pair_valid.reshape(queries, det_dev)
    cap = max(2, 2 * exp_dev * pair_count // n_exp)
    slots_all = n_exp * cap
    hits = (dest[:, None] == jnp.arange(n_exp, dtype=jnp.int32)[None, :]).astype(jnp.int32)
    before = jnp.cumsum(hits, axis=0) - hits
    rank = jnp.sum(before * hits, axis=1)
    slot = dest * cap + rank
    placement_table = (slot[None, :] == jnp.arange(slots_all, dtype=jnp.int32)[:, None]).astype(
        jnp.bfloat16
    )
    out_ids = jnp.zeros((slots_all,), jnp.int32).at[slot].set(wanted + 1).reshape(n_exp, cap)
    in_ids = lax.all_to_all(out_ids, "exp", split_axis=0, concat_axis=0, tiled=True)
    incoming = in_ids.reshape(-1)
    served_selection = (
        incoming[:, None] - 1 == jnp.arange(exp_dev, dtype=jnp.int32)[None, :]
    ).astype(jnp.bfloat16)
    owners = (incoming[None, :] - 1 == jnp.arange(exp_dev, dtype=jnp.int32)[:, None]).astype(
        jnp.bfloat16
    )
    fwd_rows = shift_mats(row_offs, pixels)
    fwd_cols = shift_mats(col_offs, pixels)
    back_rows = shift_mats(-row_offs, pixels)
    back_cols = shift_mats(-col_offs, pixels)
    intersection = intersection_masks(row_offs, col_offs, pixels).reshape(
        exp_dev, pair_count, 1, pixels, pixels
    )
    kv32 = along_rows.astype(jnp.float32)
    kh32 = along_cols.astype(jnp.float32)
    flat_norm = 1.0 / math.sqrt(2.0 * pair_count * exp_dev * n_exp)
    bkg_parts = []
    terms = None
    for dd in range(det_dev):
        sl = slice(dd, dd + 1)
        image_d = images[:, sl]
        pick_d = pick[:, sl]
        gains = jnp.einsum("edg,gpq->edpq", pick_d, all_flat, precision=high)
        calibrated = (gains * image_d.astype(jnp.float32) - backgrounds[:, sl, None, None]).astype(
            jnp.bfloat16
        )
        half_done = jnp.einsum(
            "edyw,exw->edyx", calibrated, along_cols, preferred_element_type=jnp.float32
        ).astype(jnp.bfloat16)
        matched = jnp.einsum(
            "evy,edyx->edvx", along_rows, half_done, preferred_element_type=jnp.float32
        ).astype(jnp.bfloat16)
        served = jnp.einsum(
            "lm,muqo->luqo", served_selection, matched, preferred_element_type=jnp.float32
        ).astype(jnp.bfloat16)
        served = served.reshape(n_exp, cap, 1, pixels, pixels)
        returned = lax.all_to_all(served, "exp", split_axis=0, concat_axis=0, tiled=True)
        partners = jnp.einsum(
            "fj,fvhm->jvhm",
            placement_table,
            returned.reshape(slots_all, 1, pixels, pixels),
            preferred_element_type=jnp.float32,
        ).astype(jnp.bfloat16)
        moved = apply_shift(partners, fwd_rows, fwd_cols)
        weight = valid_flat[:, sl].astype(jnp.float32).reshape(exp_dev, pair_count, 1, 1, 1)
        moved = moved.reshape(exp_dev, pair_count, 1, pixels, pixels)
        resid = weight * intersection * (matched[:, None].astype(jnp.float32) - moved)
        adj_own = jnp.sum(resid, axis=1)
        resid_low = resid.reshape(queries, 1, pixels, pixels).astype(jnp.bfloat16)
        returned_images = apply_shift(resid_low, back_rows, back_cols).astype(jnp.bfloat16)
        sending_images = jnp.einsum(
            "ea,ajhv->ejhv", placement_table, returned_images, preferred_element_type=jnp.float32
        ).astype(jnp.bfloat16)
        sending_images = sending_images.reshape(n_exp, cap, 1, pixels, pixels)
        arrived = lax.all_to_all(
            sending_images, "exp", split_axis=0, concat_axis=0, tiled=True
        ).reshape(slots_all, 1, pixels, pixels)
        adj_partner = jnp.einsum(
            "js,sdpq->jdpq", owners, arrived, preferred_element_type=jnp.float32
        )
        adj_matched = adj_own - adj_partner
        partial_rows = jnp.einsum("edyx,exw->edyw", adj_matched, kh32, precision=high)
        adj_cal = jnp.einsum("eyv,edyw->edvw", kv32, partial_rows, precision=high)
        bkg_parts.append(-jnp.sum(adj_cal, axis=(2, 3)) / pixels)
        part = jnp.einsum(
            "edg,edpq->gpq", pick_d, image_d.astype(jnp.float32) * adj_cal * flat_norm,
            precision=high,
        )
        terms = part if terms is None else terms + part
    grad_bkg = jnp.concatenate(bkg_parts, axis=1)
    band_rows = pixels // n_exp
    by_det = lax.psum_scatter(terms, "det", scatter_dimension=0, tiled=True)
    by_band = by_det.reshape(det_dev, n_exp, band_rows, pixels).transpose(1, 0, 2, 3)
    grad_flat = jnp.sum(
        lax.all_to_all(by_band, "exp", split_axis=0, concat_axis=0, tiled=True), axis=0
    )
    return (grad_flat, grad_bkg)


def solution(mesh):
    return jax.shard_map(
        body,
        mesh=mesh,
        in_specs=(
            P("exp", "det", None, None),
            P("exp", "det"),
            P("det", None, None),
            P("exp", "det"),
            P("exp", None, None),
            P("exp", None),
            P("exp", None),
            P("exp", None, None),
            P("exp", None, "det"),
        ),
        out_specs=(P("det", "exp", None), P("exp", "det")),
        check_vma=False,
    )
```

time: 613 us -> 619 us (level)
  waiting for transfers between devices: 385 us -> 305 us
  local copies, waits for them, and re-layouts: 63 us -> 106 us
  matrix products: 64 us -> 100 us
  starting transfers between devices: 49.4 us -> 60.6 us
    all_to_all x1 -> x2, waiting for transfers between devices: 177 us -> 123 us  [body(): lax.all_to_all(sending_images, 'exp', split_axis=0, concat_axis=0, tiled=...]
    all_to_all x1 -> x2, waiting for transfers between devices: 175 us -> 151 us  [body(): lax.all_to_all(served, 'exp', split_axis=0, concat_axis=0, tiled=True)]
    reshape x2 -> x5, local copies, waits for them, and re-layouts: 14 us -> 35.1 us  [the longest x2 17.5 us: body(): served = served.reshape(n_exp, cap, 1, pixels, pixels)]
    convert_element_type x4 -> x1, other arithmetic: 14.7 us -> 0.02 us  [body(): valid_flat[:, sl].astype(jnp.float32).reshape(exp_dev, pair_count, 1, 1, 1)]
    convert_element_type x3 -> x0, local copies, waits for them, and re-layouts: 11.2 us -> none  [the longest x1 6.55 us: body(): returned_images = apply_shift(resid_low, shift_mats(-row_offs, pixels), s...]
    dot_general x2 -> x4, matrix products: 21.1 us -> 31.4 us  [apply_shift(): jnp.einsum('qyu,qdux->qdyx', row_mats, partial_cols, preferred_element_ty...]
    reduce_sum x0 -> x1, other arithmetic: none -> 8.7 us  [body(): adj_own = jnp.sum(resid, axis=1)]
    all_to_all x1 -> x2, local copies, waits for them, and re-layouts: 9.39 us -> 18 us  [body(): lax.all_to_all(sending_images, 'exp', split_axis=0, concat_axis=0, tiled=...]
  transfers between devices with their start and end apart: 5 -> 7, of which waited for: 4 -> 6; matrix products, arithmetic and copies ran while one was open for 6% -> 19% of each run, Pallas kernels for 0% -> 0%
where the time goes in v2:
time: 619 us; the launch traced here: 609 us
  waiting for transfers between devices  305 us (49%)
  local copies, waits for them, and re-layouts  106 us (17%)
  matrix products  100 us (16%)
  starting transfers between devices  60.6 us (10%)
  between operations  14.9 us (2%)
  other arithmetic  11.6 us (2%)
  blocking collectives  11.2 us (2%)
    all_to_all x2, waiting for transfers between devices, body(): lax.all_to_all(served, 'exp', split_axis=0, concat_axis=0, tiled=True)  151 us
    all_to_all x2, waiting for transfers between devices, body(): lax.all_to_all(sending_images, 'exp', split_axis=0, concat_axis=0, tiled=...  123 us
    dot_general x4, matrix products, apply_shift(): jnp.einsum('qyu,qdux->qdyx', row_mats, partial_cols, preferred_element_ty...  31.4 us
    all_to_all x2, starting transfers between devices, body(): lax.all_to_all(served, 'exp', split_axis=0, concat_axis=0, tiled=True)  19.9 us
    reduce_scatter x1, waiting for transfers between devices, body(): by_det = lax.psum_scatter(terms, 'det', scatter_dimension=0, tiled=True)  19.4 us
    all_to_all x2, local copies, waits for them, and re-layouts, body(): lax.all_to_all(sending_images, 'exp', split_axis=0, concat_axis=0, tiled=...  18 us
    all_to_all x2, local copies, waits for them, and re-layouts, body(): lax.all_to_all(served, 'exp', split_axis=0, concat_axis=0, tiled=True)  17.7 us
    reshape x2, local copies, waits for them, and re-layouts, body(): served = served.reshape(n_exp, cap, 1, pixels, pixels)  17.5 us
  transfers between devices with their start and end apart: 7, of which 6 were waited for; matrix products, arithmetic and copies ran while one was open for 19% of the time, Pallas kernels for 0%

profile of v2, /device:TPU:1, one launch (start us, length us, event | category | flops | bytes accessed | tf_op | source)
XLA Modules:
  0.0 609.2 jit_solution(12399098088139130444)
XLA Ops:
  11.7 13.1 %all-to-all-start = ((s32[64,1,2]{2,1,0:T(1,128)}), s32[64,1,2]{2,1,0:T(1,128)S(1)}, u32[]{:S(2)}, u32[]{:S(2)}) async-start(s32[64,1,2]{2,1,0:T(1,128)} %bitcast.19), calls=%async_computation | async-start | bytes 65536 | tf_op jit(solution)/shard_map/all_to_all | solution.py:65
  28.8 11.2 %all_gather.3 = f32[8,128,128]{2,1,0:T(8,128)S(1)} all-gather(f32[2,128,128]{2,1,0:T(8,128)S(1)} %copy-done.5), channel_id=1, replica_groups=mesh['exp'=64,'det'=4] {'det'}, dimensions={0}, use_global_device_ids=true | all-gather | bytes 655360 | tf_op jit(solution)/shard_map/all_gather | solution.py:35
  54.5 8.8 %copy.70 = bf16[64,2,1,128,128]{4,1,3,2,0:T(2,128)(2,1)} copy(bf16[64,2,1,128,128]{4,1,0,3,2:T(2,128)(2,1)} %bitcast.188) | data formatting | bytes 8388608 | tf_op jit(solution)/shard_map/reshape | solution.py:102
  63.3 12.4 %all-to-all-start.1 = ((bf16[64,2,1,128,128]{4,1,3,2,0:T(2,128)(2,1)}), bf16[64,2,1,128,128]{4,1,3,2,0:T(2,128)(2,1)}, u32[]{:S(2)}, u32[]{:S(2)}) async-start(bf16[64,2,1,128,128]{4,1,3,2,0:T(2,128)(2,1)} %copy.70), calls=%async_computation.1 | async-start | bytes 8388608 | tf_op jit(solution)/shard_map/all_to_all | solution.py:103
  91.0 8.8 %copy.94 = bf16[64,2,1,128,128]{4,1,3,2,0:T(2,128)(2,1)} copy(bf16[64,2,1,128,128]{4,1,0,3,2:T(2,128)(2,1)} %bitcast.189) | data formatting | bytes 8388608 | tf_op jit(solution)/shard_map/reshape | solution.py:102
  99.7 70.8 %all-to-all-done.1 = bf16[64,2,1,128,128]{4,1,3,2,0:T(2,128)(2,1)} async-done(((bf16[64,2,1,128,128]{4,1,3,2,0:T(2,128)(2,1)}), bf16[64,2,1,128,128]{4,1,3,2,0:T(2,128)(2,1)}, u32[]{:S(2)}, u32[]{:S(2)}) %all-to-all-start.1) | async-done | bytes 4194336 | tf_op jit(solution)/shard_map/all_to_all | solution.py:103
  170.5 7.5 %all-to-all-start.3 = ((bf16[64,2,1,128,128]{4,1,3,2,0:T(2,128)(2,1)}), bf16[64,2,1,128,128]{4,1,3,2,0:T(2,128)(2,1)}, u32[]{:S(2)}, u32[]{:S(2)}) async-start(bf16[64,2,1,128,128]{4,1,3,2,0:T(2,128)(2,1)} %copy.94), calls=%async_computation.3 | async-start | bytes 8388608 | tf_op jit(solution)/shard_map/all_to_all | solution.py:103
  178.9 8.9 %copy.71 = bf16[64,2,1,128,128]{4,1,0,3,2:T(2,128)(2,1)} copy(bf16[64,2,1,128,128]{4,1,3,2,0:T(2,128)(2,1)} %all-to-all-done.1) | data formatting | bytes 8388608 | tf_op jit(solution)/shard_map/all_to_all | solution.py:103
  192.1 80.6 %all-to-all-done.3 = bf16[64,2,1,128,128]{4,1,3,2,0:T(2,128)(2,1)} async-done(((bf16[64,2,1,128,128]{4,1,3,2,0:T(2,128)(2,1)}), bf16[64,2,1,128,128]{4,1,3,2,0:T(2,128)(2,1)}, u32[]{:S(2)}, u32[]{:S(2)}) %all-to-all-start.3) | async-done | bytes 4194336 | tf_op jit(solution)/shard_map/all_to_all | solution.py:103
  272.7 8.9 %copy.95 = bf16[64,2,1,128,128]{4,1,0,3,2:T(2,128)(2,1)} copy(bf16[64,2,1,128,128]{4,1,3,2,0:T(2,128)(2,1)} %all-to-all-done.3) | data formatting | bytes 8388608 | tf_op jit(solution)/shard_map/all_to_all | solution.py:103
  292.5 10.1 %fusion.7 = (bf16[64,1,128,128]{2,3,0,1:T(8,128)(2,1)}, bf16[64,1,128,128]{2,3,0,1:T(8,128)(2,1)}, f32[64,128,128]{2,1,0:T(8,128)}) fusion(f32[32,128,128]{1,2,0:T(8,128)} %get-tuple-element.20, f32[64]{0:T(128)S(1)} %get-tuple-element.16, pred[64,128]{1,0:T(8,128)(4,1)S(1)} %get-tuple-element.31, pred[64,128]{1,0:T(8,128)(4,1)S(1)} %get-tuple-element.32, ...), kind=kOutput, calls=%fused_computation.12 | convolution fusion | flops 549453824 | bytes 18956800 | tf_op jit(solution)/shard_map/qyu,qdux->qdyx/dot_general | solution.py:18
  302.6 7.2 %convert_bitcast_fusion.1 = bf16[64,128,128]{1,2,0:T(8,128)(2,1)} fusion(s32[64,128]{1,0:T(8,128)S(1)} %get-tuple-element.35, bf16[64,1,128,128]{2,3,0,1:T(8,128)(2,1)} %get-tuple-element.13, s32[64,128]{1,0:T(8,128)S(1)} %get-tuple-element.36), kind=kOutput, calls=%fused_computation.58 | convolution fusion | flops 541065216 | bytes 4259840 | tf_op jit(solution)/shard_map/qyu,qdux->qdyx/dot_general | solution.py:18
  318.9 8.7 %copy.79 = bf16[64,2,1,128,128]{4,1,3,2,0:T(2,128)(2,1)} copy(bf16[64,2,1,128,128]{4,1,0,3,2:T(2,128)(2,1)} %bitcast.192) | data formatting | bytes 8388608 | tf_op jit(solution)/shard_map/reshape | solution.py:120
  327.7 7.4 %all-to-all-start.2 = ((bf16[64,2,1,128,128]{4,1,3,2,0:T(2,128)(2,1)}), bf16[64,2,1,128,128]{4,1,3,2,0:T(2,128)(2,1)}, u32[]{:S(2)}, u32[]{:S(2)}) async-start(bf16[64,2,1,128,128]{4,1,3,2,0:T(2,128)(2,1)} %copy.79), calls=%async_computation.2 | async-start | bytes 8388608 | tf_op jit(solution)/shard_map/all_to_all | solution.py:121
  335.1 7.3 %convert_bitcast_fusion = bf16[64,128,128]{1,2,0:T(8,128)(2,1)} fusion(s32[64,128]{1,0:T(8,128)S(1)} %get-tuple-element.35, bf16[64,1,128,128]{2,3,0,1:T(8,128)(2,1)} %get-tuple-element.12, s32[64,128]{1,0:T(8,128)S(1)} %get-tuple-element.36), kind=kOutput, calls=%fused_computation.55 | convolution fusion | flops 541065216 | bytes 4259840 | tf_op jit(solution)/shard_map/qyu,qdux->qdyx/dot_general | solution.py:18
  351.4 8.8 %copy.101 = bf16[64,2,1,128,128]{4,1,3,2,0:T(2,128)(2,1)} copy(bf16[64,2,1,128,128]{4,1,0,3,2:T(2,128)(2,1)} %bitcast.186) | data formatting | bytes 8388608 | tf_op jit(solution)/shard_map/reshape | solution.py:120
  360.2 69.6 %all-to-all-done.2 = bf16[64,2,1,128,128]{4,1,3,2,0:T(2,128)(2,1)} async-done(((bf16[64,2,1,128,128]{4,1,3,2,0:T(2,128)(2,1)}), bf16[64,2,1,128,128]{4,1,3,2,0:T(2,128)(2,1)}, u32[]{:S(2)}, u32[]{:S(2)}) %all-to-all-start.2) | async-done | bytes 4194336 | tf_op jit(solution)/shard_map/all_to_all | solution.py:121
  437.4 8.7 %fusion.3 = (f32[32,128,128]{1,2,0:T(8,128)}, f32[32,128,128]{1,2,0:T(8,128)}) fusion(f32[32,2,1,128,128]{3,4,1,0,2:T(8,128)} %bitcast.194, f32[32,128,128]{1,2,0:T(8,128)} %get-tuple-element.20, f32[32,2]{1,0:T(8,128)S(1)} %mul.138, pred[32,2,128]{2,1,0:T(4,128)(4,1)S(1)} %get-tuple-element.33, pred[32,2,128]{2,1,0:T(4,128)(4,1)S(1)} %get-tuple-element.34, ...), kind=kLoop, calls=%fused_computation.8 | loop fusion | flops 8388608 | bytes 16794112 | tf_op jit(solution)/shard_map/reduce_sum | solution.py:114
  452.3 9.0 %copy.80 = bf16[64,2,1,128,128]{4,1,0,3,2:T(2,128)(2,1)} copy(bf16[64,2,1,128,128]{4,1,3,2,0:T(2,128)(2,1)} %all-to-all-done.2) | data formatting | bytes 8388608 | tf_op jit(solution)/shard_map/all_to_all | solution.py:121
  478.0 53.7 %all-to-all-done.4 = bf16[64,2,1,128,128]{4,1,3,2,0:T(2,128)(2,1)} async-done(((bf16[64,2,1,128,128]{4,1,3,2,0:T(2,128)(2,1)}), bf16[64,2,1,128,128]{4,1,3,2,0:T(2,128)(2,1)}, u32[]{:S(2)}, u32[]{:S(2)}) %all-to-all-start.4) | async-done | bytes 4194336 | tf_op jit(solution)/shard_map/all_to_all | solution.py:121
  531.7 9.0 %copy.102 = bf16[64,2,1,128,128]{4,1,0,3,2:T(2,128)(2,1)} copy(bf16[64,2,1,128,128]{4,1,3,2,0:T(2,128)(2,1)} %all-to-all-done.4) | data formatting | bytes 8388608 | tf_op jit(solution)/shard_map/all_to_all | solution.py:121
  556.0 19.4 %reduce-scatter.2.cloned.1.call-done = f32[2,128,128]{2,1,0:T(8,128)} async-done(((f32[8,128,128]{2,1,0:T(8,128)}), f32[2,128,128]{2,1,0:T(8,128)}) %reduce-scatter.2.cloned.1.call-update) | async-done | bytes 131088 | tf_op jit(solution)/shard_map/reduce_scatter | solution.py:138
  577.0 13.0 %all-to-all-start.5 = ((f32[64,2,2,128]{3,1,2,0:T(2,128)}), f32[64,2,2,128]{3,1,2,0:T(2,128)S(1)}, u32[]{:S(2)}, u32[]{:S(2)}) async-start(f32[64,2,2,128]{3,1,2,0:T(2,128)} %bitcast.184), calls=%async_computation.6 | async-start | bytes 262144 | tf_op jit(solution)/shard_map/all_to_all | solution.py:141
  590.7 10.5 %all-to-all-done.5 = f32[64,2,2,128]{3,1,2,0:T(2,128)S(1)} async-done(((f32[64,2,2,128]{3,1,2,0:T(2,128)}), f32[64,2,2,128]{3,1,2,0:T(2,128)S(1)}, u32[]{:S(2)}, u32[]{:S(2)}) %all-to-all-start.5) | async-done | bytes 131104 | tf_op jit(solution)/shard_map/all_to_all | solution.py:141
  (100 shorter events, 121.0 us)
Async XLA Ops:
  11.7 38.1 %all-to-all-start = ((s32[64,1,2]{2,1,0:T(1,128)}), s32[64,1,2]{2,1,0:T(1,128)S(1)}, u32[]{:S(2)}, u32[]{:S(2)}) async-start(s32[64,1,2]{2,1,0:T(1,128)} %bitcast.19), calls=%async_computation | async-start | bytes 65536 | tf_op jit(solution)/shard_map/all_to_all | solution.py:65
  26.3 0.7 copy-start.9
  26.3 1.6 copy-start.4
  27.9 0.9 copy-start.5
  27.9 12.1 %copy-start.8 = (s32[32,2]{0,1:T(2,128)S(1)}, s32[32,2]{0,1:T(2,128)}, u32[]{:S(2)}) copy-start(s32[32,2]{0,1:T(2,128)} %param.10) | copy-start | bytes 772
  28.8 11.2 %copy-start = (bf16[32,1,128,128]{3,2,1,0:T(8,128)(2,1)}, bf16[32,1,128,128]{3,2,1,0:T(8,128)(2,1)S(1)}, u32[]{:S(2)}) copy-start(bf16[32,1,128,128]{3,2,1,0:T(8,128)(2,1)S(1)} %get-tuple-element.8) | copy-start | bytes 3145732
  40.0 2.7 copy-start.3
  63.3 107.2 %all-to-all-start.1 = ((bf16[64,2,1,128,128]{4,1,3,2,0:T(2,128)(2,1)}), bf16[64,2,1,128,128]{4,1,3,2,0:T(2,128)(2,1)}, u32[]{:S(2)}, u32[]{:S(2)}) async-start(bf16[64,2,1,128,128]{4,1,3,2,0:T(2,128)(2,1)} %copy.70), calls=%async_computation.1 | async-start | bytes 8388608 | tf_op jit(solution)/shard_map/all_to_all | solution.py:103
  99.7 78.3 %copy-start.6 = (s32[32,2,2]{0,2,1:T(2,128)S(1)}, s32[32,2,2]{0,2,1:T(2,128)}, u32[]{:S(2)}) copy-start(s32[32,2,2]{0,2,1:T(2,128)} %param.17) | copy-start | bytes 1540
  99.7 78.5 %copy-start.7 = (s32[32,2,2]{0,2,1:T(2,128)S(1)}, s32[32,2,2]{0,2,1:T(2,128)}, u32[]{:S(2)}) copy-start(s32[32,2,2]{0,2,1:T(2,128)} %param.16) | copy-start | bytes 1540
  170.5 102.2 %all-to-all-start.3 = ((bf16[64,2,1,128,128]{4,1,3,2,0:T(2,128)(2,1)}), bf16[64,2,1,128,128]{4,1,3,2,0:T(2,128)(2,1)}, u32[]{:S(2)}, u32[]{:S(2)}) async-start(bf16[64,2,1,128,128]{4,1,3,2,0:T(2,128)(2,1)} %copy.94), calls=%async_computation.3 | async-start | bytes 8388608 | tf_op jit(solution)/shard_map/all_to_all | solution.py:103
  327.7 102.1 %all-to-all-start.2 = ((bf16[64,2,1,128,128]{4,1,3,2,0:T(2,128)(2,1)}), bf16[64,2,1,128,128]{4,1,3,2,0:T(2,128)(2,1)}, u32[]{:S(2)}, u32[]{:S(2)}) async-start(bf16[64,2,1,128,128]{4,1,3,2,0:T(2,128)(2,1)} %copy.79), calls=%async_computation.2 | async-start | bytes 8388608 | tf_op jit(solution)/shard_map/all_to_all | solution.py:121
  429.8 101.9 %all-to-all-start.4 = ((bf16[64,2,1,128,128]{4,1,3,2,0:T(2,128)(2,1)}), bf16[64,2,1,128,128]{4,1,3,2,0:T(2,128)(2,1)}, u32[]{:S(2)}, u32[]{:S(2)}) async-start(bf16[64,2,1,128,128]{4,1,3,2,0:T(2,128)(2,1)} %copy.101), calls=%async_computation.4 | async-start | bytes 8388608 | tf_op jit(solution)/shard_map/all_to_all | solution.py:121
  436.8 138.6 %reduce-scatter.2.cloned.1.call-start = ((), (), s32[]{:S(2)}) async-start(), calls=%async_computation.7 | async-start | bytes 655360 | tf_op jit(solution)/shard_map/reduce_scatter | solution.py:138
  452.3 9.0 %copy-start.2 = (f32[32,128,128]{2,0,1:T(8,128)S(1)}, f32[32,128,128]{2,0,1:T(8,128)}, u32[]{:S(2)}) copy-start(f32[32,128,128]{2,0,1:T(8,128)} %copy.81) | copy-start | bytes 6291460
  531.7 9.0 %copy-start.1 = (f32[32,128,128]{2,0,1:T(8,128)S(1)}, f32[32,128,128]{2,0,1:T(8,128)}, u32[]{:S(2)}) copy-start(f32[32,128,128]{2,0,1:T(8,128)} %copy.103) | copy-start | bytes 6291460
  577.0 24.1 %all-to-all-start.5 = ((f32[64,2,2,128]{3,1,2,0:T(2,128)}), f32[64,2,2,128]{3,1,2,0:T(2,128)S(1)}, u32[]{:S(2)}, u32[]{:S(2)}) async-start(f32[64,2,2,128]{3,1,2,0:T(2,128)} %bitcast.184), calls=%async_computation.6 | async-start | bytes 262144 | tf_op jit(solution)/shard_map/all_to_all | solution.py:141
Sparse Core Ops, SparseCore 0:
  556.1 19.2 reduce-scatter.1

commit v3 on v2

--- a/solution.py
+++ b/solution.py
@@ -99,7 +99,7 @@
         served = jnp.einsum(
             "lm,muqo->luqo", served_selection, matched, preferred_element_type=jnp.float32
         ).astype(jnp.bfloat16)
-        served = served.reshape(n_exp, cap, 1, pixels, pixels)
+        served = served.reshape(n_exp, cap * pixels, pixels)
         returned = lax.all_to_all(served, "exp", split_axis=0, concat_axis=0, tiled=True)
         partners = jnp.einsum(
             "fj,fvhm->jvhm",
@@ -117,7 +117,7 @@
         sending_images = jnp.einsum(
             "ea,ajhv->ejhv", placement_table, returned_images, preferred_element_type=jnp.float32
         ).astype(jnp.bfloat16)
-        sending_images = sending_images.reshape(n_exp, cap, 1, pixels, pixels)
+        sending_images = sending_images.reshape(n_exp, cap * pixels, pixels)
         arrived = lax.all_to_all(
             sending_images, "exp", split_axis=0, concat_axis=0, tiled=True
         ).reshape(slots_all, 1, pixels, pixels)

time: 619 us -> 593 us (0.958)
  local copies, waits for them, and re-layouts: 106 us -> 53.6 us
  waiting for transfers between devices: 305 us -> 330 us
    all_to_all x4 -> x0, local copies, waits for them, and re-layouts: 35.7 us -> none  [the longest x2 18 us: body(): lax.all_to_all(sending_images, 'exp', split_axis=0, concat_axis=0, tiled=...]
    reshape x4 -> x0, local copies, waits for them, and re-layouts: 35 us -> none  [the longest x2 17.5 us: body(): served = served.reshape(n_exp, cap, 1, pixels, pixels)]
    convert_element_type x0 -> x4, local copies, waits for them, and re-layouts: none -> 18.6 us  [the longest x2 9.31 us: body(): served = jnp.einsum('lm,muqo->luqo', served_selection, matched, preferred...]
    all_to_all x2, waiting for transfers between devices: 151 us -> 164 us  [body(): lax.all_to_all(served, 'exp', split_axis=0, concat_axis=0, tiled=True)]
    all_to_all x2, waiting for transfers between devices: 123 us -> 136 us  [body(): lax.all_to_all(sending_images, 'exp', split_axis=0, concat_axis=0, tiled=...]
  transfers between devices with their start and end apart: 7 -> 7, of which waited for: 6 -> 6; matrix products, arithmetic and copies ran while one was open for 19% -> 16% of each run, Pallas kernels for 0% -> 0%
where the time goes in v3:
time: 593 us; the launch traced here: 583 us
  waiting for transfers between devices  330 us (56%)
  matrix products  102 us (17%)
  starting transfers between devices  60.7 us (10%)
  local copies, waits for them, and re-layouts  53.6 us (9%)
  between operations  14.6 us (2%)
  other arithmetic  11.9 us (2%)
  blocking collectives  11.2 us (2%)
    all_to_all x2, waiting for transfers between devices, body(): lax.all_to_all(served, 'exp', split_axis=0, concat_axis=0, tiled=True)  164 us
    all_to_all x2, waiting for transfers between devices, body(): lax.all_to_all(sending_images, 'exp', split_axis=0, concat_axis=0, tiled=...  136 us
    dot_general x4, matrix products, apply_shift(): jnp.einsum('qyu,qdux->qdyx', row_mats, partial_cols, preferred_element_ty...  31 us
    all_to_all x2, starting transfers between devices, body(): lax.all_to_all(served, 'exp', split_axis=0, concat_axis=0, tiled=True)  20 us
    reduce_scatter x1, waiting for transfers between devices, body(): by_det = lax.psum_scatter(terms, 'det', scatter_dimension=0, tiled=True)  19.4 us
    all_to_all x2, starting transfers between devices, body(): lax.all_to_all(sending_images, 'exp', split_axis=0, concat_axis=0, tiled=...  14.5 us
    all_to_all x1, starting transfers between devices, body(): lax.all_to_all(out_ids, 'exp', split_axis=0, concat_axis=0, tiled=True)  13.1 us
    all_to_all x1, starting transfers between devices, body(): lax.all_to_all(by_band, 'exp', split_axis=0, concat_axis=0, tiled=True)  13 us
  transfers between devices with their start and end apart: 7, of which 6 were waited for; matrix products, arithmetic and copies ran while one was open for 16% of the time, Pallas kernels for 0%

profile of v3, /device:TPU:1, one launch (start us, length us, event | category | flops | bytes accessed | tf_op | source)
XLA Modules:
  0.0 583.2 jit_solution(217336974365360922)
XLA Ops:
  11.7 13.1 %all-to-all-start = ((s32[64,1,2]{2,1,0:T(1,128)}), s32[64,1,2]{2,1,0:T(1,128)S(1)}, u32[]{:S(2)}, u32[]{:S(2)}) async-start(s32[64,1,2]{2,1,0:T(1,128)} %bitcast.19), calls=%async_computation | async-start | bytes 65536 | tf_op jit(solution)/shard_map/all_to_all | solution.py:65
  28.8 11.2 %all_gather.3 = f32[8,128,128]{2,1,0:T(8,128)S(1)} all-gather(f32[2,128,128]{2,1,0:T(8,128)S(1)} %copy-done.3), channel_id=1, replica_groups=mesh['exp'=64,'det'=4] {'det'}, dimensions={0}, use_global_device_ids=true | all-gather | bytes 655360 | tf_op jit(solution)/shard_map/all_gather | solution.py:35
  52.5 4.7 copy.127
  57.2 12.4 %all-to-all-start.1 = ((bf16[64,256,128]{2,1,0:T(8,128)(2,1)}), bf16[64,256,128]{2,1,0:T(8,128)(2,1)}, u32[]{:S(2)}, u32[]{:S(2)}) async-start(bf16[64,256,128]{2,1,0:T(8,128)(2,1)} %bitcast.183), calls=%async_computation.1 | async-start | bytes 8388608 | tf_op jit(solution)/shard_map/all_to_all | solution.py:103
  82.9 4.6 copy.151
  87.6 76.8 %all-to-all-done.1 = bf16[64,256,128]{2,1,0:T(8,128)(2,1)} async-done(((bf16[64,256,128]{2,1,0:T(8,128)(2,1)}), bf16[64,256,128]{2,1,0:T(8,128)(2,1)}, u32[]{:S(2)}, u32[]{:S(2)}) %all-to-all-start.1) | async-done | bytes 4194336 | tf_op jit(solution)/shard_map/all_to_all | solution.py:103
  164.4 7.6 %all-to-all-start.3 = ((bf16[64,256,128]{2,1,0:T(8,128)(2,1)}), bf16[64,256,128]{2,1,0:T(8,128)(2,1)}, u32[]{:S(2)}, u32[]{:S(2)}) async-start(bf16[64,256,128]{2,1,0:T(8,128)(2,1)} %bitcast.182), calls=%async_computation.3 | async-start | bytes 8388608 | tf_op jit(solution)/shard_map/all_to_all | solution.py:103
  172.9 6.5 %fusion.86 = bf16[64,128,128]{2,0,1:T(8,128)(2,1)} fusion(bf16[128,128,128]{2,1,0:T(8,128)(2,1)} %bitcast.24, s32[64]{0:T(128)S(1)} %multiply_add_fusion), kind=kOutput, calls=%fused_computation.78 | convolution fusion | flops 269492224 | bytes 6291712 | tf_op jit(solution)/shard_map/fj,fvhm->jvhm/dot_general | solution.py:104
  179.4 87.3 %all-to-all-done.3 = bf16[64,256,128]{2,1,0:T(8,128)(2,1)} async-done(((bf16[64,256,128]{2,1,0:T(8,128)(2,1)}), bf16[64,256,128]{2,1,0:T(8,128)(2,1)}, u32[]{:S(2)}, u32[]{:S(2)}) %all-to-all-start.3) | async-done | bytes 4194336 | tf_op jit(solution)/shard_map/all_to_all | solution.py:103
  266.6 6.5 %fusion.89 = bf16[64,128,128]{2,0,1:T(8,128)(2,1)} fusion(bf16[128,128,128]{2,1,0:T(8,128)(2,1)} %bitcast.52, s32[64]{0:T(128)S(1)} %multiply_add_fusion), kind=kOutput, calls=%fused_computation.79 | convolution fusion | flops 269492224 | bytes 6291712 | tf_op jit(solution)/shard_map/fj,fvhm->jvhm/dot_general | solution.py:104
  273.1 6.7 %fusion.21 = f32[64,128,128]{2,1,0:T(8,128)} fusion(s32[64,128]{1,0:T(8,128)S(1)} %get-tuple-element.31, bf16[64,128,128]{2,0,1:T(8,128)(2,1)} %fusion.86, s32[64,128]{1,0:T(8,128)S(1)} %get-tuple-element.32), kind=kOutput, calls=%fused_computation.31 | convolution fusion | flops 540016640 | bytes 6356992 | tf_op jit(solution)/shard_map/qyu,qdux->qdyx/dot_general | solution.py:18
  279.8 9.6 %fusion.7 = (bf16[64,1,128,128]{2,3,0,1:T(8,128)(2,1)}, bf16[64,1,128,128]{2,3,0,1:T(8,128)(2,1)}, f32[64,128,128]{2,1,0:T(8,128)}) fusion(f32[32,128,128]{1,2,0:T(8,128)} %get-tuple-element.22, f32[64]{0:T(128)S(1)} %get-tuple-element.18, pred[64,128]{1,0:T(8,128)(4,1)S(1)} %get-tuple-element.33, pred[64,128]{1,0:T(8,128)(4,1)S(1)} %get-tuple-element.34, ...), kind=kOutput, calls=%fused_computation.12 | convolution fusion | flops 549453824 | bytes 18956800 | tf_op jit(solution)/shard_map/qyu,qdux->qdyx/dot_general | solution.py:18
  289.4 7.5 %convert_bitcast_fusion.1 = bf16[64,128,128]{1,2,0:T(8,128)(2,1)} fusion(s32[64,128]{1,0:T(8,128)S(1)} %get-tuple-element.37, bf16[64,1,128,128]{2,3,0,1:T(8,128)(2,1)} %get-tuple-element.15, s32[64,128]{1,0:T(8,128)S(1)} %get-tuple-element.38), kind=kOutput, calls=%fused_computation.66 | convolution fusion | flops 541065216 | bytes 4259840 | tf_op jit(solution)/shard_map/qyu,qdux->qdyx/dot_general | solution.py:18
  308.6 7.5 %all-to-all-start.2 = ((bf16[64,256,128]{2,1,0:T(8,128)(2,1)}), bf16[64,256,128]{2,1,0:T(8,128)(2,1)}, u32[]{:S(2)}, u32[]{:S(2)}) async-start(bf16[64,256,128]{2,1,0:T(8,128)(2,1)} %bitcast.184), calls=%async_computation.2 | async-start | bytes 8388608 | tf_op jit(solution)/shard_map/all_to_all | solution.py:121
  316.1 7.3 %convert_bitcast_fusion = bf16[64,128,128]{1,2,0:T(8,128)(2,1)} fusion(s32[64,128]{1,0:T(8,128)S(1)} %get-tuple-element.37, bf16[64,1,128,128]{2,3,0,1:T(8,128)(2,1)} %get-tuple-element.14, s32[64,128]{1,0:T(8,128)S(1)} %get-tuple-element.38), kind=kOutput, calls=%fused_computation.63 | convolution fusion | flops 541065216 | bytes 4259840 | tf_op jit(solution)/shard_map/qyu,qdux->qdyx/dot_general | solution.py:18
  335.1 75.7 %all-to-all-done.2 = bf16[64,256,128]{2,1,0:T(8,128)(2,1)} async-done(((bf16[64,256,128]{2,1,0:T(8,128)(2,1)}), bf16[64,256,128]{2,1,0:T(8,128)(2,1)}, u32[]{:S(2)}, u32[]{:S(2)}) %all-to-all-start.2) | async-done | bytes 4194336 | tf_op jit(solution)/shard_map/all_to_all | solution.py:121
  410.8 7.0 %all-to-all-start.4 = ((bf16[64,256,128]{2,1,0:T(8,128)(2,1)}), bf16[64,256,128]{2,1,0:T(8,128)(2,1)}, u32[]{:S(2)}, u32[]{:S(2)}) async-start(bf16[64,256,128]{2,1,0:T(8,128)(2,1)} %bitcast.181), calls=%async_computation.4 | async-start | bytes 8388608 | tf_op jit(solution)/shard_map/all_to_all | solution.py:121
  418.4 8.9 %fusion.3 = (f32[32,128,128]{1,2,0:T(8,128)}, f32[32,128,128]{1,2,0:T(8,128)}) fusion(f32[32,2,1,128,128]{3,4,1,0,2:T(8,128)} %bitcast.186, f32[32,128,128]{1,2,0:T(8,128)} %get-tuple-element.22, f32[32,2]{1,0:T(8,128)S(1)} %mul.138, pred[32,2,128]{2,1,0:T(4,128)(4,1)S(1)} %get-tuple-element.35, pred[32,2,128]{2,1,0:T(4,128)(4,1)S(1)} %get-tuple-element.36, ...), kind=kLoop, calls=%fused_computation.8 | loop fusion | flops 8388608 | bytes 16794112 | tf_op jit(solution)/shard_map/reduce_sum | solution.py:114
  433.6 5.5 fusion.92
  452.7 59.9 %all-to-all-done.4 = bf16[64,256,128]{2,1,0:T(8,128)(2,1)} async-done(((bf16[64,256,128]{2,1,0:T(8,128)(2,1)}), bf16[64,256,128]{2,1,0:T(8,128)(2,1)}, u32[]{:S(2)}, u32[]{:S(2)}) %all-to-all-start.4) | async-done | bytes 4194336 | tf_op jit(solution)/shard_map/all_to_all | solution.py:121
  512.7 5.5 fusion.95
  530.3 19.4 %reduce-scatter.2.cloned.1.call-done = f32[2,128,128]{2,1,0:T(8,128)} async-done(((f32[8,128,128]{2,1,0:T(8,128)}), f32[2,128,128]{2,1,0:T(8,128)}) %reduce-scatter.2.cloned.1.call-update) | async-done | bytes 131088 | tf_op jit(solution)/shard_map/reduce_scatter | solution.py:138
  551.3 13.0 %all-to-all-start.5 = ((f32[64,2,2,128]{3,1,2,0:T(2,128)}), f32[64,2,2,128]{3,1,2,0:T(2,128)S(1)}, u32[]{:S(2)}, u32[]{:S(2)}) async-start(f32[64,2,2,128]{3,1,2,0:T(2,128)} %bitcast.180), calls=%async_computation.6 | async-start | bytes 262144 | tf_op jit(solution)/shard_map/all_to_all | solution.py:141
  565.0 10.5 %all-to-all-done.5 = f32[64,2,2,128]{3,1,2,0:T(2,128)S(1)} async-done(((f32[64,2,2,128]{3,1,2,0:T(2,128)}), f32[64,2,2,128]{3,1,2,0:T(2,128)S(1)}, u32[]{:S(2)}, u32[]{:S(2)}) %all-to-all-start.5) | async-done | bytes 131104 | tf_op jit(solution)/shard_map/all_to_all | solution.py:141
  (92 shorter events, 94.0 us)
Async XLA Ops:
  11.7 38.1 %all-to-all-start = ((s32[64,1,2]{2,1,0:T(1,128)}), s32[64,1,2]{2,1,0:T(1,128)S(1)}, u32[]{:S(2)}, u32[]{:S(2)}) async-start(s32[64,1,2]{2,1,0:T(1,128)} %bitcast.19), calls=%async_computation | async-start | bytes 65536 | tf_op jit(solution)/shard_map/all_to_all | solution.py:65
  26.3 0.7 copy-start.7
  26.3 1.6 copy-start.2
  27.9 0.9 copy-start.3
  27.9 12.1 %copy-start.6 = (s32[32,2]{0,1:T(2,128)S(1)}, s32[32,2]{0,1:T(2,128)}, u32[]{:S(2)}) copy-start(s32[32,2]{0,1:T(2,128)} %param.10) | copy-start | bytes 772
  28.8 11.2 %copy-start = (bf16[32,1,128,128]{3,2,1,0:T(8,128)(2,1)}, bf16[32,1,128,128]{3,2,1,0:T(8,128)(2,1)S(1)}, u32[]{:S(2)}) copy-start(bf16[32,1,128,128]{3,2,1,0:T(8,128)(2,1)S(1)} %get-tuple-element.10) | copy-start | bytes 3145732
  40.0 2.7 copy-start.1
  57.2 107.2 %all-to-all-start.1 = ((bf16[64,256,128]{2,1,0:T(8,128)(2,1)}), bf16[64,256,128]{2,1,0:T(8,128)(2,1)}, u32[]{:S(2)}, u32[]{:S(2)}) async-start(bf16[64,256,128]{2,1,0:T(8,128)(2,1)} %bitcast.183), calls=%async_computation.1 | async-start | bytes 8388608 | tf_op jit(solution)/shard_map/all_to_all | solution.py:103
  164.4 7.6 %copy-start.4 = (s32[32,2,2]{0,2,1:T(2,128)S(1)}, s32[32,2,2]{0,2,1:T(2,128)}, u32[]{:S(2)}) copy-start(s32[32,2,2]{0,2,1:T(2,128)} %param.17) | copy-start | bytes 1540
  164.4 7.8 %copy-start.5 = (s32[32,2,2]{0,2,1:T(2,128)S(1)}, s32[32,2,2]{0,2,1:T(2,128)}, u32[]{:S(2)}) copy-start(s32[32,2,2]{0,2,1:T(2,128)} %param.16) | copy-start | bytes 1540
  164.4 102.3 %all-to-all-start.3 = ((bf16[64,256,128]{2,1,0:T(8,128)(2,1)}), bf16[64,256,128]{2,1,0:T(8,128)(2,1)}, u32[]{:S(2)}, u32[]{:S(2)}) async-start(bf16[64,256,128]{2,1,0:T(8,128)(2,1)} %bitcast.182), calls=%async_computation.3 | async-start | bytes 8388608 | tf_op jit(solution)/shard_map/all_to_all | solution.py:103
  308.6 102.2 %all-to-all-start.2 = ((bf16[64,256,128]{2,1,0:T(8,128)(2,1)}), bf16[64,256,128]{2,1,0:T(8,128)(2,1)}, u32[]{:S(2)}, u32[]{:S(2)}) async-start(bf16[64,256,128]{2,1,0:T(8,128)(2,1)} %bitcast.184), calls=%async_computation.2 | async-start | bytes 8388608 | tf_op jit(solution)/shard_map/all_to_all | solution.py:121
  410.8 101.9 %all-to-all-start.4 = ((bf16[64,256,128]{2,1,0:T(8,128)(2,1)}), bf16[64,256,128]{2,1,0:T(8,128)(2,1)}, u32[]{:S(2)}, u32[]{:S(2)}) async-start(bf16[64,256,128]{2,1,0:T(8,128)(2,1)} %bitcast.181), calls=%async_computation.4 | async-start | bytes 8388608 | tf_op jit(solution)/shard_map/all_to_all | solution.py:121
  417.8 131.9 %reduce-scatter.2.cloned.1.call-start = ((), (), s32[]{:S(2)}) async-start(), calls=%async_computation.7 | async-start | bytes 655360 | tf_op jit(solution)/shard_map/reduce_scatter | solution.py:138
  551.3 24.1 %all-to-all-start.5 = ((f32[64,2,2,128]{3,1,2,0:T(2,128)}), f32[64,2,2,128]{3,1,2,0:T(2,128)S(1)}, u32[]{:S(2)}, u32[]{:S(2)}) async-start(f32[64,2,2,128]{3,1,2,0:T(2,128)} %bitcast.180), calls=%async_computation.6 | async-start | bytes 262144 | tf_op jit(solution)/shard_map/all_to_all | solution.py:141
Sparse Core Ops, SparseCore 0:
  530.4 19.2 reduce-scatter.1

commit v4 on v1

--- a/solution.py
+++ b/solution.py
@@ -100,7 +100,7 @@
     served_flat = jnp.einsum(
         "lm,muqo->luqo", served_selection, psf_matched_images, preferred_element_type=jnp.float32
     ).astype(jnp.bfloat16)
-    served = served_flat.reshape(n_exp, cap, det_dev, pixels, pixels)
+    served = served_flat.reshape(n_exp, cap * det_dev * pixels, pixels)
     returned = lax.all_to_all(served, "exp", split_axis=0, concat_axis=0, tiled=True)
     partners = jnp.einsum(
         "fj,fvhm->jvhm",
@@ -123,7 +123,7 @@
     sending_images = jnp.einsum(
         "ea,ajhv->ejhv", placement_table, returned_images, preferred_element_type=jnp.float32
     ).astype(jnp.bfloat16)
-    sending_images = sending_images.reshape(n_exp, cap, det_dev, pixels, pixels)
+    sending_images = sending_images.reshape(n_exp, cap * det_dev * pixels, pixels)
     arrived = lax.all_to_all(
         sending_images, "exp", split_axis=0, concat_axis=0, tiled=True
     ).reshape(slots_all, det_dev, pixels, pixels)
@@ -143,11 +143,16 @@
     terms = jnp.einsum(
         "edg,edpq->gpq", pick, images.astype(jnp.float32) * adj_cal * flat_norm, precision=high
     )
-    by_det = lax.psum_scatter(terms, "det", scatter_dimension=0, tiled=True)
     band_rows = pixels // n_exp
-    by_band = by_det.reshape(det_dev, n_exp, band_rows, pixels).transpose(1, 0, 2, 3)
+    n_det = det_total // det_dev
+    by_block = (
+        terms.reshape(n_det, det_dev, n_exp, band_rows, pixels)
+        .transpose(2, 0, 1, 3, 4)
+        .reshape(n_exp * n_det, det_dev, band_rows, pixels)
+    )
     grad_flat = jnp.sum(
-        lax.all_to_all(by_band, "exp", split_axis=0, concat_axis=0, tiled=True), axis=0
+        lax.all_to_all(by_block, ("exp", "det"), split_axis=0, concat_axis=0, tiled=True),
+        axis=0,
     )
     return (grad_flat, grad_bkg)
 

time: 613 us -> 598 us (0.976)
  matrix products: 64 us -> 87.1 us
  waiting for transfers between devices: 385 us -> 370 us
  between operations: 14.8 us -> 1.1 us
  local copies, waits for them, and re-layouts: 63 us -> 53.1 us
    convert_element_type x0 -> x2, local copies, waits for them, and re-layouts: none -> 24 us  [the longest x1 12 us: body(): served_flat = jnp.einsum('lm,muqo->luqo', served_selection, psf_matched_i...]
    reduce_scatter x1 -> x0, waiting for transfers between devices: 22.7 us -> none  [body(): by_det = lax.psum_scatter(terms, 'det', scatter_dimension=0, tiled=True)]
    all_to_all x2 -> x0, local copies, waits for them, and re-layouts: 18.6 us -> none  [the longest x1 9.39 us: body(): lax.all_to_all(sending_images, 'exp', split_axis=0, concat_axis=0, tiled=...]
    reshape x3 -> x2, local copies, waits for them, and re-layouts: 15.7 us -> 1.34 us  [the longest x1 1.2 us: body(): by_block = terms.reshape(n_det, det_dev, n_exp, band_rows, pixels).transp...]
    all_to_all x1, waiting for transfers between devices: 10.4 us -> 19.2 us  [body(): lax.all_to_all(by_block, ('exp', 'det'), split_axis=0, concat_axis=0, til...]
    dot_general x1, matrix products: 1.24 us -> 9.84 us  [body(): jnp.einsum('js,sdpq->jdpq', owners, arrived, preferred_element_type=jnp.f...]
    dot_general x1, matrix products: 3.26 us -> 11.2 us  [body(): jnp.einsum('fj,fvhm->jvhm', placement_table, returned.reshape(slots_all,...]
  transfers between devices with their start and end apart: 5 -> 4, of which waited for: 4 -> 3; matrix products, arithmetic and copies ran while one was open for 6% -> 6% of each run, Pallas kernels for 0% -> 0%
where the time goes in v4:
time: 598 us; the launch traced here: 591 us
  waiting for transfers between devices  370 us (62%)
  matrix products  87.1 us (15%)
  local copies, waits for them, and re-layouts  53.1 us (9%)
  starting transfers between devices  50.1 us (8%)
  other arithmetic  17.8 us (3%)
  blocking collectives  11.1 us (2%)
    all_to_all x1, waiting for transfers between devices, body(): lax.all_to_all(sending_images, 'exp', split_axis=0, concat_axis=0, tiled=...  176 us
    all_to_all x1, waiting for transfers between devices, body(): lax.all_to_all(served, 'exp', split_axis=0, concat_axis=0, tiled=True)  175 us
    dot_general x2, matrix products, apply_shift(): jnp.einsum('qyu,qdux->qdyx', row_mats, partial_cols, preferred_element_ty...  21.1 us
    all_to_all x1, waiting for transfers between devices, body(): lax.all_to_all(by_block, ('exp', 'det'), split_axis=0, concat_axis=0, til...  19.2 us
    all_to_all x1, starting transfers between devices, body(): lax.all_to_all(out_ids, 'exp', split_axis=0, concat_axis=0, tiled=True)  13.1 us
    all_to_all x1, starting transfers between devices, body(): lax.all_to_all(served, 'exp', split_axis=0, concat_axis=0, tiled=True)  13.1 us
    all_to_all x1, starting transfers between devices, body(): lax.all_to_all(by_block, ('exp', 'det'), split_axis=0, concat_axis=0, til...  12.8 us
    convert_element_type x1, local copies, waits for them, and re-layouts, body(): served_flat = jnp.einsum('lm,muqo->luqo', served_selection, psf_matched_i...  12 us
  transfers between devices with their start and end apart: 4, of which 3 were waited for; matrix products, arithmetic and copies ran while one was open for 6% of the time, Pallas kernels for 0%

profile of v4, /device:TPU:1, one launch (start us, length us, event | category | flops | bytes accessed | tf_op | source)
XLA Modules:
  0.0 590.5 jit_solution(9526965976825037709)
XLA Ops:
  5.3 13.1 %all-to-all-start = ((s32[64,1,2]{2,1,0:T(1,128)}), s32[64,1,2]{2,1,0:T(1,128)S(1)}, u32[]{:S(2)}, u32[]{:S(2)}) async-start(s32[64,1,2]{2,1,0:T(1,128)} %bitcast.18), calls=%async_computation | async-start | bytes 65536 | tf_op jit(solution)/shard_map/all_to_all | solution.py:90
  20.4 11.1 %all_gather.3 = f32[8,128,128]{2,1,0:T(8,128)S(1)} all-gather(f32[2,128,128]{2,1,0:T(8,128)S(1)} %copy-done.2), channel_id=1, replica_groups=mesh['exp'=64,'det'=4] {'det'}, dimensions={0}, use_global_device_ids=true | all-gather | bytes 655360 | tf_op jit(solution)/shard_map/all_gather | solution.py:37
  31.5 7.6 %fusion.7 = bf16[32,2,128,128]{3,0,2,1:T(8,128)(2,1)} fusion(f32[32,2]{0,1:T(2,128)S(1)} %copy-done.6, bf16[32,2,128,128]{3,2,1,0:T(8,128)(2,1)S(1)} %copy-done, f32[8,128,128]{2,1,0:T(8,128)S(1)} %all_gather.3, s32[32,2]{0,1:T(2,128)S(1)} %copy-done.3), kind=kOutput, calls=%fused_computation.14 | convolution fusion | flops 104858112 | bytes 4719104 | tf_op jit(solution)/shard_map/edg,gpq->edpq/dot_general | solution.py:42
  39.1 6.1 %fusion.108 = (f32[32,2,128,128]{2,3,1,0:T(8,128)}, bf16[32,2,128,128]{2,3,1,0:T(8,128)(2,1)}) fusion(bf16[32,128,128,1]{2,0,1,3:T(8,128)(2,1)S(1)} %get-tuple-element.7, bf16[32,2,128,128]{3,0,2,1:T(8,128)(2,1)} %fusion.7, bf16[32,128,128,1]{2,0,1,3:T(8,128)(2,1)S(1)} %get-tuple-element.6), kind=kOutput, calls=%fused_computation.105 | convolution fusion | flops 540016640 | bytes 10485760 | tf_op jit(solution)/shard_map/evy,edyx->edvx/dot_general | solution.py:59
  45.2 5.1 copy.99
  50.6 7.2 %convolution_convert_fusion.1 = bf16[128,2,128,128]{3,0,2,1:T(8,128)(2,1)} fusion(bf16[32,2,128,128]{3,0,2,1:T(8,128)(2,1)} %copy.99, s32[128]{0:T(128)S(1)} %sub.60), kind=kOutput, calls=%fused_computation.10 | convolution fusion | flops 272633856 | bytes 10486272 | tf_op jit(solution)/shard_map/lm,muqo->luqo/dot_general | solution.py:100
  57.8 12.0 %copy.100 = bf16[128,2,128,128]{3,2,1,0:T(8,128)(2,1)} copy(bf16[128,2,128,128]{3,0,2,1:T(8,128)(2,1)} %convolution_convert_fusion.1) | data formatting | bytes 16777216 | tf_op jit(solution)/shard_map/convert_element_type | solution.py:102
  69.8 13.1 %all-to-all-start.1 = ((bf16[64,512,128]{2,1,0:T(8,128)(2,1)}), bf16[64,512,128]{2,1,0:T(8,128)(2,1)}, u32[]{:S(2)}, u32[]{:S(2)}) async-start(bf16[64,512,128]{2,1,0:T(8,128)(2,1)} %bitcast.136), calls=%async_computation.1 | async-start | bytes 16777216 | tf_op jit(solution)/shard_map/all_to_all | solution.py:104
  90.1 174.7 %all-to-all-done.1 = bf16[64,512,128]{2,1,0:T(8,128)(2,1)} async-done(((bf16[64,512,128]{2,1,0:T(8,128)(2,1)}), bf16[64,512,128]{2,1,0:T(8,128)(2,1)}, u32[]{:S(2)}, u32[]{:S(2)}) %all-to-all-start.1) | async-done | bytes 8388640 | tf_op jit(solution)/shard_map/all_to_all | solution.py:104
  264.8 11.2 %fusion.47 = bf16[64,2,128,128]{3,0,2,1:T(8,128)(2,1)} fusion(bf16[128,2,128,128]{3,2,1,0:T(8,128)(2,1)} %bitcast.22, s32[64]{0:T(128)S(1)} %multiply_add_fusion), kind=kOutput, calls=%fused_computation.39 | convolution fusion | flops 538976256 | bytes 12583168 | tf_op jit(solution)/shard_map/fj,fvhm->jvhm/dot_general | solution.py:105
  276.0 13.0 %multiply_reduce_fusion = (f32[32,2,128,128]{2,3,1,0:T(8,128)}, f32[64,2,128,128]{3,2,1,0:T(8,128)}) fusion(f32[32,2,128,128]{2,3,1,0:T(8,128)} %get-tuple-element.10, f32[32,2,128,128]{2,3,1,0:T(8,128)} %and_convert_fusion.1, f32[32,2,2]{2,1,0:T(2,128)S(1)} %copy.86, s32[64,128]{1,0:T(8,128)S(1)} %get-tuple-element.18, ...), kind=kOutput, calls=%fused_computation.8 | convolution fusion | flops 1085276160 | bytes 25231872 | tf_op jit(solution)/shard_map/qyu,qdux->qdyx/dot_general | solution.py:18
  289.0 8.6 %fusion.1 = bf16[64,2,128,128]{2,3,1,0:T(8,128)(2,1)} fusion(f32[64,2,128,128]{3,2,1,0:T(8,128)} %get-tuple-element.13, f32[64,128,128]{1,2,0:T(8,128)} %and_convert_fusion, f32[64,2]{1,0:T(8,128)S(1)} %bitcast.140, f32[32,2,128,128]{2,3,1,0:T(8,128)} %get-tuple-element.10), kind=kLoop, calls=%fused_computation.3 | loop fusion | flops 8388608 | bytes 20972032 | tf_op jit(solution)/shard_map/convert_element_type | solution.py:119
  297.6 8.1 %convert_bitcast_fusion = bf16[64,2,128,128]{2,3,1,0:T(8,128)(2,1)} fusion(bf16[64,2,128,128]{2,3,1,0:T(8,128)(2,1)} %fusion.1, s32[64,128]{1,0:T(8,128)S(1)} %get-tuple-element.22, s32[64,128]{1,0:T(8,128)S(1)} %get-tuple-element.23), kind=kOutput, calls=%fused_computation.23 | convolution fusion | flops 1080033280 | bytes 8454144 | tf_op jit(solution)/shard_map/qyu,qdux->qdyx/dot_general | solution.py:18
  305.7 6.8 %copy.110 = bf16[64,2,128,128]{3,0,2,1:T(8,128)(2,1)} copy(bf16[64,2,128,128]{2,3,1,0:T(8,128)(2,1)} %convert_bitcast_fusion) | data formatting | bytes 8388608 | tf_op jit(solution)/shard_map/convert_element_type | solution.py:122
  312.5 7.8 %convolution_convert_fusion = bf16[128,2,128,128]{3,0,2,1:T(8,128)(2,1)} fusion(bf16[64,2,128,128]{3,0,2,1:T(8,128)(2,1)} %copy.110, s32[64]{0:T(128)S(1)} %multiply_add_fusion), kind=kOutput, calls=%fused_computation.9 | convolution fusion | flops 541073408 | bytes 12583168 | tf_op jit(solution)/shard_map/ea,ajhv->ejhv/dot_general | solution.py:123
  320.3 12.0 %copy.111 = bf16[128,2,128,128]{3,2,1,0:T(8,128)(2,1)} copy(bf16[128,2,128,128]{3,0,2,1:T(8,128)(2,1)} %convolution_convert_fusion) | data formatting | bytes 16777216 | tf_op jit(solution)/shard_map/convert_element_type | solution.py:125
  332.3 11.1 %all-to-all-start.2 = ((bf16[64,512,128]{2,1,0:T(8,128)(2,1)}), bf16[64,512,128]{2,1,0:T(8,128)(2,1)}, u32[]{:S(2)}, u32[]{:S(2)}) async-start(bf16[64,512,128]{2,1,0:T(8,128)(2,1)} %bitcast.137), calls=%async_computation.2 | async-start | bytes 16777216 | tf_op jit(solution)/shard_map/all_to_all | solution.py:127
  343.4 5.5 copy.113
  348.9 176.4 %all-to-all-done.2 = bf16[64,512,128]{2,1,0:T(8,128)(2,1)} async-done(((bf16[64,512,128]{2,1,0:T(8,128)(2,1)}), bf16[64,512,128]{2,1,0:T(8,128)(2,1)}, u32[]{:S(2)}, u32[]{:S(2)}) %all-to-all-start.2) | async-done | bytes 8388640 | tf_op jit(solution)/shard_map/all_to_all | solution.py:127
  525.3 9.8 %fusion.65 = f32[32,2,128,128]{3,0,2,1:T(8,128)S(1)} fusion(f32[32,2,128,128]{3,0,2,1:T(8,128)} %copy.113, bf16[128,2,128,128]{3,2,1,0:T(8,128)(2,1)} %bitcast.40, s32[128]{0:T(128)S(1)} %sub.60), kind=kOutput, calls=%fused_computation.51 | convolution fusion | flops 269488128 | bytes 16777728 | tf_op jit(solution)/shard_map/js,sdpq->jdpq/dot_general | solution.py:133
  535.2 5.2 fusion.12
  544.9 5.6 copy.118
  556.8 12.8 %all-to-all-start.3 = ((f32[256,2,2,128]{3,2,1,0:T(2,128)}), f32[256,2,2,128]{3,2,1,0:T(2,128)S(1)}, u32[]{:S(2)}, u32[]{:S(2)}) async-start(f32[256,2,2,128]{3,2,1,0:T(2,128)} %copy.121), calls=%async_computation.3 | async-start | bytes 1048576 | tf_op jit(solution)/shard_map/all_to_all | solution.py:154
  570.3 19.2 %all-to-all-done.3 = f32[256,2,2,128]{3,2,1,0:T(2,128)S(1)} async-done(((f32[256,2,2,128]{3,2,1,0:T(2,128)}), f32[256,2,2,128]{3,2,1,0:T(2,128)S(1)}, u32[]{:S(2)}, u32[]{:S(2)}) %all-to-all-start.3) | async-done | bytes 524320 | tf_op jit(solution)/shard_map/all_to_all | solution.py:154
  (59 shorter events, 26.2 us)
Async XLA Ops:
  0.6 19.8 %copy-start.2 = (f32[2,128,128]{2,1,0:T(8,128)S(1)}, f32[2,128,128]{2,1,0:T(8,128)}, u32[]{:S(2)}) copy-start(f32[2,128,128]{2,1,0:T(8,128)} %param.11) | copy-start | bytes 393220
  0.6 30.8 %copy-start.3 = (s32[32,2]{0,1:T(2,128)S(1)}, s32[32,2]{0,1:T(2,128)}, u32[]{:S(2)}) copy-start(s32[32,2]{0,1:T(2,128)} %param.10) | copy-start | bytes 772
  0.7 30.8 %copy-start.6 = (f32[32,2]{0,1:T(2,128)S(1)}, f32[32,2]{0,1:T(2,128)}, u32[]{:S(2)}) copy-start(f32[32,2]{0,1:T(2,128)} %param.12) | copy-start | bytes 772
  5.3 45.1 %all-to-all-start = ((s32[64,1,2]{2,1,0:T(1,128)}), s32[64,1,2]{2,1,0:T(1,128)S(1)}, u32[]{:S(2)}, u32[]{:S(2)}) async-start(s32[64,1,2]{2,1,0:T(1,128)} %bitcast.18), calls=%async_computation | async-start | bytes 65536 | tf_op jit(solution)/shard_map/all_to_all | solution.py:90
  18.4 13.1 %copy-start = (bf16[32,2,128,128]{3,2,1,0:T(8,128)(2,1)S(1)}, bf16[32,2,128,128]{3,2,1,0:T(8,128)(2,1)}, u32[]{:S(2)}) copy-start(bf16[32,2,128,128]{3,2,1,0:T(8,128)(2,1)} %param.9) | copy-start | bytes 6291460
  69.8 13.1 %copy-start.4 = (s32[32,2,2]{0,2,1:T(2,128)S(1)}, s32[32,2,2]{0,2,1:T(2,128)}, u32[]{:S(2)}) copy-start(s32[32,2,2]{0,2,1:T(2,128)} %param.16) | copy-start | bytes 1540
  69.8 13.7 %copy-start.5 = (s32[32,2,2]{0,2,1:T(2,128)S(1)}, s32[32,2,2]{0,2,1:T(2,128)}, u32[]{:S(2)}) copy-start(s32[32,2,2]{0,2,1:T(2,128)} %param.17) | copy-start | bytes 1540
  69.8 195.0 %all-to-all-start.1 = ((bf16[64,512,128]{2,1,0:T(8,128)(2,1)}), bf16[64,512,128]{2,1,0:T(8,128)(2,1)}, u32[]{:S(2)}, u32[]{:S(2)}) async-start(bf16[64,512,128]{2,1,0:T(8,128)(2,1)} %bitcast.136), calls=%async_computation.1 | async-start | bytes 16777216 | tf_op jit(solution)/shard_map/all_to_all | solution.py:104
  332.3 193.0 %all-to-all-start.2 = ((bf16[64,512,128]{2,1,0:T(8,128)(2,1)}), bf16[64,512,128]{2,1,0:T(8,128)(2,1)}, u32[]{:S(2)}, u32[]{:S(2)}) async-start(bf16[64,512,128]{2,1,0:T(8,128)(2,1)} %bitcast.137), calls=%async_computation.2 | async-start | bytes 16777216 | tf_op jit(solution)/shard_map/all_to_all | solution.py:127
  544.9 5.6 copy-start.1
  556.8 32.7 %all-to-all-start.3 = ((f32[256,2,2,128]{3,2,1,0:T(2,128)}), f32[256,2,2,128]{3,2,1,0:T(2,128)S(1)}, u32[]{:S(2)}, u32[]{:S(2)}) async-start(f32[256,2,2,128]{3,2,1,0:T(2,128)} %copy.121), calls=%async_computation.3 | async-start | bytes 1048576 | tf_op jit(solution)/shard_map/all_to_all | solution.py:154

commit v5 on v4

--- a/solution.py
+++ b/solution.py
@@ -97,17 +97,24 @@
     served_selection = (
         incoming[:, None] - 1 == jnp.arange(exp_dev, dtype=jnp.int32)[None, :]
     ).astype(jnp.bfloat16)
-    served_flat = jnp.einsum(
-        "lm,muqo->luqo", served_selection, psf_matched_images, preferred_element_type=jnp.float32
+    image_elems = det_dev * pixels * pixels
+    served_flat = jnp.dot(
+        served_selection,
+        psf_matched_images.reshape(exp_dev, image_elems),
+        preferred_element_type=jnp.float32,
     ).astype(jnp.bfloat16)
     served = served_flat.reshape(n_exp, cap * det_dev * pixels, pixels)
     returned = lax.all_to_all(served, "exp", split_axis=0, concat_axis=0, tiled=True)
-    partners = jnp.einsum(
-        "fj,fvhm->jvhm",
-        placement_table,
-        returned.reshape(slots_all, det_dev, pixels, pixels),
-        preferred_element_type=jnp.float32,
-    ).astype(jnp.bfloat16)
+    partners = (
+        lax.dot_general(
+            placement_table,
+            returned.reshape(slots_all, image_elems),
+            (((0,), (0,)), ((), ())),
+            preferred_element_type=jnp.float32,
+        )
+        .astype(jnp.bfloat16)
+        .reshape(queries, det_dev, pixels, pixels)
+    )
     moved = apply_shift(partners, shift_mats(row_offs, pixels), shift_mats(col_offs, pixels))
     intersection = intersection_masks(row_offs, col_offs, pixels).reshape(
         exp_dev, pair_count, 1, pixels, pixels
@@ -120,17 +127,21 @@
     returned_images = apply_shift(
         resid_low, shift_mats(-row_offs, pixels), shift_mats(-col_offs, pixels)
     ).astype(jnp.bfloat16)
-    sending_images = jnp.einsum(
-        "ea,ajhv->ejhv", placement_table, returned_images, preferred_element_type=jnp.float32
+    sending_images = jnp.dot(
+        placement_table,
+        returned_images.reshape(queries, image_elems),
+        preferred_element_type=jnp.float32,
     ).astype(jnp.bfloat16)
     sending_images = sending_images.reshape(n_exp, cap * det_dev * pixels, pixels)
     arrived = lax.all_to_all(
         sending_images, "exp", split_axis=0, concat_axis=0, tiled=True
-    ).reshape(slots_all, det_dev, pixels, pixels)
+    ).reshape(slots_all, image_elems)
     owners = (incoming[None, :] - 1 == jnp.arange(exp_dev, dtype=jnp.int32)[:, None]).astype(
         jnp.bfloat16
     )
-    adj_partner = jnp.einsum("js,sdpq->jdpq", owners, arrived, preferred_element_type=jnp.float32)
+    adj_partner = jnp.dot(owners, arrived, preferred_element_type=jnp.float32).reshape(
+        exp_dev, det_dev, pixels, pixels
+    )
     adj_matched = adj_own - adj_partner
     partial_rows = jnp.einsum(
         "edyx,exw->edyw", adj_matched, along_cols.astype(jnp.float32), precision=high

time: 598 us -> 635 us (1.062)
  local copies, waits for them, and re-layouts: 53.1 us -> 96.4 us
  matrix products: 87.1 us -> 77.9 us
    reshape x0 -> x5, local copies, waits for them, and re-layouts: none -> 65.5 us  [the longest x2 25.2 us: body(): arrived = lax.all_to_all(sending_images, 'exp', split_axis=0, concat_axis...]
    convert_element_type x2 -> x0, local copies, waits for them, and re-layouts: 24 us -> none  [the longest x1 12 us: body(): served_flat = jnp.einsum('lm,muqo->luqo', served_selection, psf_matched_i...]
    dot_general x4, matrix products: 36.1 us -> 28 us  [the longest x1 8.75 us: body(): jnp.dot(placement_table, returned_images.reshape(queries, image_elems), p...]
  transfers between devices with their start and end apart: 4 -> 4, of which waited for: 3 -> 3; matrix products, arithmetic and copies ran while one was open for 6% -> 5% of each run, Pallas kernels for 0% -> 0%
where the time goes in v5:
time: 635 us; the launch traced here: 624 us
  waiting for transfers between devices  371 us (58%)
  local copies, waits for them, and re-layouts  96.4 us (15%)
  matrix products  77.9 us (12%)
  starting transfers between devices  49.3 us (8%)
  other arithmetic  17.8 us (3%)
  blocking collectives  11.1 us (2%)
    all_to_all x1, waiting for transfers between devices, body(): lax.all_to_all(sending_images, 'exp', split_axis=0, concat_axis=0, tiled=...  177 us
    all_to_all x1, waiting for transfers between devices, body(): lax.all_to_all(served, 'exp', split_axis=0, concat_axis=0, tiled=True)  175 us
    reshape x2, local copies, waits for them, and re-layouts, body(): arrived = lax.all_to_all(sending_images, 'exp', split_axis=0, concat_axis...  25.2 us
    dot_general x2, matrix products, apply_shift(): jnp.einsum('qyu,qdux->qdyx', row_mats, partial_cols, preferred_element_ty...  20 us
    all_to_all x1, waiting for transfers between devices, body(): lax.all_to_all(by_block, ('exp', 'det'), split_axis=0, concat_axis=0, til...  19.2 us
    reshape x1, local copies, waits for them, and re-layouts, body(): served = served_flat.reshape(n_exp, cap * det_dev * pixels, pixels)  13.5 us
    reshape x1, local copies, waits for them, and re-layouts, body(): sending_images.reshape(n_exp, cap * det_dev * pixels, pixels)  13.5 us
    reshape x1, local copies, waits for them, and re-layouts, body(): returned.reshape(slots_all, image_elems)  13.3 us
  transfers between devices with their start and end apart: 4, of which 3 were waited for; matrix products, arithmetic and copies ran while one was open for 5% of the time, Pallas kernels for 0%

profile of v5, /device:TPU:1, one launch (start us, length us, event | category | flops | bytes accessed | tf_op | source)
XLA Modules:
  0.0 624.3 jit_solution(4716634106634923618)
XLA Ops:
  5.3 13.1 %all-to-all-start = ((s32[64,1,2]{2,1,0:T(1,128)}), s32[64,1,2]{2,1,0:T(1,128)S(1)}, u32[]{:S(2)}, u32[]{:S(2)}) async-start(s32[64,1,2]{2,1,0:T(1,128)} %bitcast.16), calls=%async_computation | async-start | bytes 65536 | tf_op jit(solution)/shard_map/all_to_all | solution.py:90
  20.4 11.1 %all_gather.3 = f32[8,128,128]{2,1,0:T(8,128)S(1)} all-gather(f32[2,128,128]{2,1,0:T(8,128)S(1)} %copy-done.2), channel_id=1, replica_groups=mesh['exp'=64,'det'=4] {'det'}, dimensions={0}, use_global_device_ids=true | all-gather | bytes 655360 | tf_op jit(solution)/shard_map/all_gather | solution.py:37
  31.5 7.6 %fusion.3 = bf16[32,2,128,128]{3,0,2,1:T(8,128)(2,1)} fusion(f32[32,2]{0,1:T(2,128)S(1)} %copy-done.6, bf16[32,2,128,128]{3,2,1,0:T(8,128)(2,1)S(1)} %copy-done, f32[8,128,128]{2,1,0:T(8,128)S(1)} %all_gather.3, s32[32,2]{0,1:T(2,128)S(1)} %copy-done.3), kind=kOutput, calls=%fused_computation.11 | convolution fusion | flops 104858112 | bytes 4719104 | tf_op jit(solution)/shard_map/edg,gpq->edpq/dot_general | solution.py:42
  39.1 6.1 fusion.93
  49.5 7.2 %convolution_convert_fusion.1 = bf16[128,32768]{1,0:T(8,128)(2,1)} fusion(bf16[4,8,256,128]{3,2,1,0:T(8,128)(2,1)} %bitcast.142, s32[128]{0:T(128)S(1)} %sub.60), kind=kOutput, calls=%fused_computation.2 | convolution fusion | flops 272633856 | bytes 10486272 | tf_op jit(solution)/shard_map/dot_general | solution.py:101
  56.7 13.5 %reshape.301 = bf16[64,512,128]{2,1,0:T(8,128)(2,1)} reshape(bf16[128,32768]{1,0:T(8,128)(2,1)} %convolution_convert_fusion.1) | data formatting | bytes 16777216 | tf_op jit(solution)/shard_map/reshape | solution.py:106
  70.2 13.0 %all-to-all-start.1 = ((bf16[64,512,128]{2,1,0:T(8,128)(2,1)}), bf16[64,512,128]{2,1,0:T(8,128)(2,1)}, u32[]{:S(2)}, u32[]{:S(2)}) async-start(bf16[64,512,128]{2,1,0:T(8,128)(2,1)} %reshape.301), calls=%async_computation.1 | async-start | bytes 16777216 | tf_op jit(solution)/shard_map/all_to_all | solution.py:107
  90.5 174.7 %all-to-all-done.1 = bf16[64,512,128]{2,1,0:T(8,128)(2,1)} async-done(((bf16[64,512,128]{2,1,0:T(8,128)(2,1)}), bf16[64,512,128]{2,1,0:T(8,128)(2,1)}, u32[]{:S(2)}, u32[]{:S(2)}) %all-to-all-start.1) | async-done | bytes 8388640 | tf_op jit(solution)/shard_map/all_to_all | solution.py:107
  265.1 13.3 %reshape.302 = bf16[128,32768]{1,0:T(8,128)(2,1)} reshape(bf16[64,512,128]{2,1,0:T(8,128)(2,1)} %all-to-all-done.1) | data formatting | bytes 16777216 | tf_op jit(solution)/shard_map/reshape | solution.py:111
  286.2 11.9 %multiply_reduce_fusion = (f32[32,2,128,128]{2,3,1,0:T(8,128)}, f32[64,2,128,128]{3,2,1,0:T(8,128)}) fusion(f32[32,2,128,128]{2,3,1,0:T(8,128)} %get-tuple-element.8, f32[32,2,128,128]{2,3,1,0:T(8,128)} %and_convert_fusion.1, f32[32,2,2]{2,1,0:T(2,128)S(1)} %copy.47, s32[64,128]{1,0:T(8,128)S(1)} %get-tuple-element.16, ...), kind=kOutput, calls=%fused_computation.7 | convolution fusion | flops 1085276160 | bytes 25231872 | tf_op jit(solution)/shard_map/qyu,qdux->qdyx/dot_general | solution.py:18
  298.1 8.6 %fusion.1 = bf16[64,2,128,128]{2,3,1,0:T(8,128)(2,1)} fusion(f32[64,2,128,128]{3,2,1,0:T(8,128)} %get-tuple-element.11, f32[64,128,128]{1,2,0:T(8,128)} %and_convert_fusion, f32[64,2]{1,0:T(8,128)S(1)} %bitcast.145, f32[32,2,128,128]{2,3,1,0:T(8,128)} %get-tuple-element.8), kind=kLoop, calls=%fused_computation.6 | loop fusion | flops 8388608 | bytes 20972032 | tf_op jit(solution)/shard_map/convert_element_type | solution.py:126
  306.7 8.1 %convert_bitcast_fusion = bf16[64,2,128,128]{2,3,1,0:T(8,128)(2,1)} fusion(bf16[64,2,128,128]{2,3,1,0:T(8,128)(2,1)} %fusion.1, s32[64,128]{1,0:T(8,128)S(1)} %get-tuple-element.20, s32[64,128]{1,0:T(8,128)S(1)} %get-tuple-element.21), kind=kOutput, calls=%fused_computation.20 | convolution fusion | flops 1080033280 | bytes 8454144 | tf_op jit(solution)/shard_map/qyu,qdux->qdyx/dot_general | solution.py:18
  314.8 6.3 %copy.68 = bf16[64,2,128,128]{3,2,1,0:T(8,128)(2,1)} copy(bf16[64,2,128,128]{2,3,1,0:T(8,128)(2,1)} %convert_bitcast_fusion) | data formatting | bytes 8388608 | tf_op jit(solution)/shard_map/convert_element_type | solution.py:129
  321.2 8.8 %convolution_convert_fusion = bf16[128,32768]{1,0:T(8,128)(2,1)} fusion(bf16[8,8,256,128]{3,2,1,0:T(8,128)(2,1)} %bitcast.140, s32[64]{0:T(128)S(1)} %multiply_add_fusion), kind=kOutput, calls=%fused_computation.1 | convolution fusion | flops 541073408 | bytes 12583168 | tf_op jit(solution)/shard_map/dot_general | solution.py:130
  329.9 13.5 %reshape.306 = bf16[64,512,128]{2,1,0:T(8,128)(2,1)} reshape(bf16[128,32768]{1,0:T(8,128)(2,1)} %convolution_convert_fusion) | data formatting | bytes 16777216 | tf_op jit(solution)/shard_map/reshape | solution.py:135
  343.4 10.5 %all-to-all-start.2 = ((bf16[64,512,128]{2,1,0:T(8,128)(2,1)}), bf16[64,512,128]{2,1,0:T(8,128)(2,1)}, u32[]{:S(2)}, u32[]{:S(2)}) async-start(bf16[64,512,128]{2,1,0:T(8,128)(2,1)} %reshape.306), calls=%async_computation.2 | async-start | bytes 16777216 | tf_op jit(solution)/shard_map/all_to_all | solution.py:136
  353.8 5.5 copy.70
  359.4 176.8 %all-to-all-done.2 = bf16[64,512,128]{2,1,0:T(8,128)(2,1)} async-done(((bf16[64,512,128]{2,1,0:T(8,128)(2,1)}), bf16[64,512,128]{2,1,0:T(8,128)(2,1)}, u32[]{:S(2)}, u32[]{:S(2)}) %all-to-all-start.2) | async-done | bytes 8388640 | tf_op jit(solution)/shard_map/all_to_all | solution.py:136
  536.1 13.3 %reshape.307 = bf16[128,32768]{1,0:T(8,128)(2,1)} reshape(bf16[64,512,128]{2,1,0:T(8,128)(2,1)} %all-to-all-done.2) | data formatting | bytes 16777216 | tf_op jit(solution)/shard_map/reshape | solution.py:138
  549.4 11.9 %copy.69 = bf16[128,32768]{0,1:T(8,128)(2,1)} copy(bf16[128,32768]{1,0:T(8,128)(2,1)} %reshape.307) | data formatting | bytes 16777216 | tf_op jit(solution)/shard_map/reshape | solution.py:138
  561.4 7.4 %convolution_subtract_fusion = f32[32,2,128,128]{3,0,2,1:T(8,128)S(1)} fusion(f32[32,2,128,128]{3,0,2,1:T(8,128)} %copy.70, bf16[2,128,128,128]{3,2,1,0:T(8,128)(2,1)} %bitcast.139, s32[128]{0:T(128)S(1)} %sub.60), kind=kOutput, calls=%fused_computation.38 | convolution fusion | flops 269488128 | bytes 16777728 | tf_op jit(solution)/shard_map/dot_general | solution.py:142
  578.4 5.9 copy.75
  590.6 12.6 %all-to-all-start.3 = ((f32[256,2,2,128]{3,2,1,0:T(2,128)}), f32[256,2,2,128]{3,2,1,0:T(2,128)S(1)}, u32[]{:S(2)}, u32[]{:S(2)}) async-start(f32[256,2,2,128]{3,2,1,0:T(2,128)} %copy.78), calls=%async_computation.3 | async-start | bytes 1048576 | tf_op jit(solution)/shard_map/all_to_all | solution.py:165
  603.8 19.2 %all-to-all-done.3 = f32[256,2,2,128]{3,2,1,0:T(2,128)S(1)} async-done(((f32[256,2,2,128]{3,2,1,0:T(2,128)}), f32[256,2,2,128]{3,2,1,0:T(2,128)S(1)}, u32[]{:S(2)}, u32[]{:S(2)}) %all-to-all-start.3) | async-done | bytes 524320 | tf_op jit(solution)/shard_map/all_to_all | solution.py:165
  (63 shorter events, 43.1 us)
Async XLA Ops:
  0.6 19.8 %copy-start.2 = (f32[2,128,128]{2,1,0:T(8,128)S(1)}, f32[2,128,128]{2,1,0:T(8,128)}, u32[]{:S(2)}) copy-start(f32[2,128,128]{2,1,0:T(8,128)} %param.11) | copy-start | bytes 393220
  0.6 30.8 %copy-start.3 = (s32[32,2]{0,1:T(2,128)S(1)}, s32[32,2]{0,1:T(2,128)}, u32[]{:S(2)}) copy-start(s32[32,2]{0,1:T(2,128)} %param.10) | copy-start | bytes 772
  0.7 30.8 %copy-start.6 = (f32[32,2]{0,1:T(2,128)S(1)}, f32[32,2]{0,1:T(2,128)}, u32[]{:S(2)}) copy-start(f32[32,2]{0,1:T(2,128)} %param.12) | copy-start | bytes 772
  5.3 44.0 %all-to-all-start = ((s32[64,1,2]{2,1,0:T(1,128)}), s32[64,1,2]{2,1,0:T(1,128)S(1)}, u32[]{:S(2)}, u32[]{:S(2)}) async-start(s32[64,1,2]{2,1,0:T(1,128)} %bitcast.16), calls=%async_computation | async-start | bytes 65536 | tf_op jit(solution)/shard_map/all_to_all | solution.py:90
  18.4 13.1 %copy-start = (bf16[32,2,128,128]{3,2,1,0:T(8,128)(2,1)S(1)}, bf16[32,2,128,128]{3,2,1,0:T(8,128)(2,1)}, u32[]{:S(2)}) copy-start(bf16[32,2,128,128]{3,2,1,0:T(8,128)(2,1)} %param.9) | copy-start | bytes 6291460
  70.2 13.1 %copy-start.4 = (s32[32,2,2]{0,2,1:T(2,128)S(1)}, s32[32,2,2]{0,2,1:T(2,128)}, u32[]{:S(2)}) copy-start(s32[32,2,2]{0,2,1:T(2,128)} %param.16) | copy-start | bytes 1540
  70.2 13.6 %copy-start.5 = (s32[32,2,2]{0,2,1:T(2,128)S(1)}, s32[32,2,2]{0,2,1:T(2,128)}, u32[]{:S(2)}) copy-start(s32[32,2,2]{0,2,1:T(2,128)} %param.17) | copy-start | bytes 1540
  70.2 195.0 %all-to-all-start.1 = ((bf16[64,512,128]{2,1,0:T(8,128)(2,1)}), bf16[64,512,128]{2,1,0:T(8,128)(2,1)}, u32[]{:S(2)}, u32[]{:S(2)}) async-start(bf16[64,512,128]{2,1,0:T(8,128)(2,1)} %reshape.301), calls=%async_computation.1 | async-start | bytes 16777216 | tf_op jit(solution)/shard_map/all_to_all | solution.py:107
  343.4 192.8 %all-to-all-start.2 = ((bf16[64,512,128]{2,1,0:T(8,128)(2,1)}), bf16[64,512,128]{2,1,0:T(8,128)(2,1)}, u32[]{:S(2)}, u32[]{:S(2)}) async-start(bf16[64,512,128]{2,1,0:T(8,128)(2,1)} %reshape.306), calls=%async_computation.2 | async-start | bytes 16777216 | tf_op jit(solution)/shard_map/all_to_all | solution.py:136
  578.4 5.9 copy-start.1
  590.6 32.5 %all-to-all-start.3 = ((f32[256,2,2,128]{3,2,1,0:T(2,128)}), f32[256,2,2,128]{3,2,1,0:T(2,128)S(1)}, u32[]{:S(2)}, u32[]{:S(2)}) async-start(f32[256,2,2,128]{3,2,1,0:T(2,128)} %copy.78), calls=%async_computation.3 | async-start | bytes 1048576 | tf_op jit(solution)/shard_map/all_to_all | solution.py:165

commit v6 on v3

--- a/solution.py
+++ b/solution.py
@@ -135,10 +135,15 @@
         terms = part if terms is None else terms + part
     grad_bkg = jnp.concatenate(bkg_parts, axis=1)
     band_rows = pixels // n_exp
-    by_det = lax.psum_scatter(terms, "det", scatter_dimension=0, tiled=True)
-    by_band = by_det.reshape(det_dev, n_exp, band_rows, pixels).transpose(1, 0, 2, 3)
+    n_det = det_total // det_dev
+    by_block = (
+        terms.reshape(n_det, det_dev, n_exp, band_rows, pixels)
+        .transpose(2, 0, 1, 3, 4)
+        .reshape(n_exp * n_det, det_dev, band_rows, pixels)
+    )
     grad_flat = jnp.sum(
-        lax.all_to_all(by_band, "exp", split_axis=0, concat_axis=0, tiled=True), axis=0
+        lax.all_to_all(by_block, ("exp", "det"), split_axis=0, concat_axis=0, tiled=True),
+        axis=0,
     )
     return (grad_flat, grad_bkg)
 

time: 593 us -> 565 us (0.953)
  between operations: 14.6 us -> 1.18 us
  waiting for transfers between devices: 330 us -> 319 us
    reduce_scatter x1 -> x0, waiting for transfers between devices: 19.4 us -> none  [body(): by_det = lax.psum_scatter(terms, 'det', scatter_dimension=0, tiled=True)]
    all_to_all x1, waiting for transfers between devices: 10.5 us -> 19.3 us  [body(): lax.all_to_all(by_block, ('exp', 'det'), split_axis=0, concat_axis=0, til...]
  transfers between devices with their start and end apart: 7 -> 6, of which waited for: 6 -> 5; matrix products, arithmetic and copies ran while one was open for 16% -> 16% of each run, Pallas kernels for 0% -> 0%
where the time goes in v6:
time: 565 us; the launch traced here: 555 us
  waiting for transfers between devices  319 us (56%)
  matrix products  102 us (18%)
  starting transfers between devices  58.2 us (10%)
  local copies, waits for them, and re-layouts  51.8 us (9%)
  other arithmetic  12.2 us (2%)
  blocking collectives  11.2 us (2%)
    all_to_all x2, waiting for transfers between devices, body(): lax.all_to_all(served, 'exp', split_axis=0, concat_axis=0, tiled=True)  164 us
    all_to_all x2, waiting for transfers between devices, body(): lax.all_to_all(sending_images, 'exp', split_axis=0, concat_axis=0, tiled=...  136 us
    dot_general x4, matrix products, apply_shift(): jnp.einsum('qyu,qdux->qdyx', row_mats, partial_cols, preferred_element_ty...  31 us
    all_to_all x2, starting transfers between devices, body(): lax.all_to_all(served, 'exp', split_axis=0, concat_axis=0, tiled=True)  20.7 us
    all_to_all x1, waiting for transfers between devices, body(): lax.all_to_all(by_block, ('exp', 'det'), split_axis=0, concat_axis=0, til...  19.3 us
    all_to_all x2, starting transfers between devices, body(): lax.all_to_all(sending_images, 'exp', split_axis=0, concat_axis=0, tiled=...  15.1 us
    all_to_all x1, starting transfers between devices, body(): lax.all_to_all(out_ids, 'exp', split_axis=0, concat_axis=0, tiled=True)  13.1 us
    dot_general x2, matrix products, body(): jnp.einsum('fj,fvhm->jvhm', placement_table, returned.reshape(slots_all,...  12.9 us
  transfers between devices with their start and end apart: 6, of which 5 were waited for; matrix products, arithmetic and copies ran while one was open for 16% of the time, Pallas kernels for 0%

profile of v6, /device:TPU:1, one launch (start us, length us, event | category | flops | bytes accessed | tf_op | source)
XLA Modules:
  0.0 555.3 jit_solution(16775723866051088381)
XLA Ops:
  5.2 13.1 %all-to-all-start = ((s32[64,1,2]{2,1,0:T(1,128)}), s32[64,1,2]{2,1,0:T(1,128)S(1)}, u32[]{:S(2)}, u32[]{:S(2)}) async-start(s32[64,1,2]{2,1,0:T(1,128)} %bitcast.19), calls=%async_computation | async-start | bytes 65536 | tf_op jit(solution)/shard_map/all_to_all | solution.py:65
  22.3 11.2 %all_gather.3 = f32[8,128,128]{2,1,0:T(8,128)S(1)} all-gather(f32[2,128,128]{2,1,0:T(8,128)S(1)} %copy-done.3), channel_id=1, replica_groups=mesh['exp'=64,'det'=4] {'det'}, dimensions={0}, use_global_device_ids=true | all-gather | bytes 655360 | tf_op jit(solution)/shard_map/all_gather | solution.py:35
  46.0 4.7 copy.127
  50.7 13.1 %all-to-all-start.1 = ((bf16[64,256,128]{2,1,0:T(8,128)(2,1)}), bf16[64,256,128]{2,1,0:T(8,128)(2,1)}, u32[]{:S(2)}, u32[]{:S(2)}) async-start(bf16[64,256,128]{2,1,0:T(8,128)(2,1)} %bitcast.183), calls=%async_computation.1 | async-start | bytes 8388608 | tf_op jit(solution)/shard_map/all_to_all | solution.py:103
  77.1 4.6 copy.151
  81.7 76.6 %all-to-all-done.1 = bf16[64,256,128]{2,1,0:T(8,128)(2,1)} async-done(((bf16[64,256,128]{2,1,0:T(8,128)(2,1)}), bf16[64,256,128]{2,1,0:T(8,128)(2,1)}, u32[]{:S(2)}, u32[]{:S(2)}) %all-to-all-start.1) | async-done | bytes 4194336 | tf_op jit(solution)/shard_map/all_to_all | solution.py:103
  158.3 7.6 %all-to-all-start.3 = ((bf16[64,256,128]{2,1,0:T(8,128)(2,1)}), bf16[64,256,128]{2,1,0:T(8,128)(2,1)}, u32[]{:S(2)}, u32[]{:S(2)}) async-start(bf16[64,256,128]{2,1,0:T(8,128)(2,1)} %bitcast.182), calls=%async_computation.3 | async-start | bytes 8388608 | tf_op jit(solution)/shard_map/all_to_all | solution.py:103
  166.8 6.5 %fusion.86 = bf16[64,128,128]{2,0,1:T(8,128)(2,1)} fusion(bf16[128,128,128]{2,1,0:T(8,128)(2,1)} %bitcast.24, s32[64]{0:T(128)S(1)} %multiply_add_fusion), kind=kOutput, calls=%fused_computation.78 | convolution fusion | flops 269492224 | bytes 6291712 | tf_op jit(solution)/shard_map/fj,fvhm->jvhm/dot_general | solution.py:104
  173.3 87.3 %all-to-all-done.3 = bf16[64,256,128]{2,1,0:T(8,128)(2,1)} async-done(((bf16[64,256,128]{2,1,0:T(8,128)(2,1)}), bf16[64,256,128]{2,1,0:T(8,128)(2,1)}, u32[]{:S(2)}, u32[]{:S(2)}) %all-to-all-start.3) | async-done | bytes 4194336 | tf_op jit(solution)/shard_map/all_to_all | solution.py:103
  260.6 6.5 %fusion.89 = bf16[64,128,128]{2,0,1:T(8,128)(2,1)} fusion(bf16[128,128,128]{2,1,0:T(8,128)(2,1)} %bitcast.52, s32[64]{0:T(128)S(1)} %multiply_add_fusion), kind=kOutput, calls=%fused_computation.79 | convolution fusion | flops 269492224 | bytes 6291712 | tf_op jit(solution)/shard_map/fj,fvhm->jvhm/dot_general | solution.py:104
  267.0 6.7 %fusion.21 = f32[64,128,128]{2,1,0:T(8,128)} fusion(s32[64,128]{1,0:T(8,128)S(1)} %get-tuple-element.27, bf16[64,128,128]{2,0,1:T(8,128)(2,1)} %fusion.86, s32[64,128]{1,0:T(8,128)S(1)} %get-tuple-element.28), kind=kOutput, calls=%fused_computation.31 | convolution fusion | flops 540016640 | bytes 6356992 | tf_op jit(solution)/shard_map/qyu,qdux->qdyx/dot_general | solution.py:18
  273.7 9.6 %fusion.7 = (bf16[64,1,128,128]{2,3,0,1:T(8,128)(2,1)}, bf16[64,1,128,128]{2,3,0,1:T(8,128)(2,1)}, f32[64,128,128]{2,1,0:T(8,128)}) fusion(f32[32,128,128]{1,2,0:T(8,128)} %get-tuple-element.18, f32[64]{0:T(128)S(1)} %get-tuple-element.14, pred[64,128]{1,0:T(8,128)(4,1)S(1)} %get-tuple-element.29, pred[64,128]{1,0:T(8,128)(4,1)S(1)} %get-tuple-element.30, ...), kind=kOutput, calls=%fused_computation.12 | convolution fusion | flops 549453824 | bytes 18956800 | tf_op jit(solution)/shard_map/qyu,qdux->qdyx/dot_general | solution.py:18
  283.3 7.5 %convert_bitcast_fusion.1 = bf16[64,128,128]{1,2,0:T(8,128)(2,1)} fusion(s32[64,128]{1,0:T(8,128)S(1)} %get-tuple-element.33, bf16[64,1,128,128]{2,3,0,1:T(8,128)(2,1)} %get-tuple-element.11, s32[64,128]{1,0:T(8,128)S(1)} %get-tuple-element.34), kind=kOutput, calls=%fused_computation.66 | convolution fusion | flops 541065216 | bytes 4259840 | tf_op jit(solution)/shard_map/qyu,qdux->qdyx/dot_general | solution.py:18
  302.5 7.4 %all-to-all-start.2 = ((bf16[64,256,128]{2,1,0:T(8,128)(2,1)}), bf16[64,256,128]{2,1,0:T(8,128)(2,1)}, u32[]{:S(2)}, u32[]{:S(2)}) async-start(bf16[64,256,128]{2,1,0:T(8,128)(2,1)} %bitcast.184), calls=%async_computation.2 | async-start | bytes 8388608 | tf_op jit(solution)/shard_map/all_to_all | solution.py:121
  310.0 7.3 %convert_bitcast_fusion = bf16[64,128,128]{1,2,0:T(8,128)(2,1)} fusion(s32[64,128]{1,0:T(8,128)S(1)} %get-tuple-element.33, bf16[64,1,128,128]{2,3,0,1:T(8,128)(2,1)} %get-tuple-element.10, s32[64,128]{1,0:T(8,128)S(1)} %get-tuple-element.34), kind=kOutput, calls=%fused_computation.63 | convolution fusion | flops 541065216 | bytes 4259840 | tf_op jit(solution)/shard_map/qyu,qdux->qdyx/dot_general | solution.py:18
  324.3 4.6 copy.158
  329.0 75.7 %all-to-all-done.2 = bf16[64,256,128]{2,1,0:T(8,128)(2,1)} async-done(((bf16[64,256,128]{2,1,0:T(8,128)(2,1)}), bf16[64,256,128]{2,1,0:T(8,128)(2,1)}, u32[]{:S(2)}, u32[]{:S(2)}) %all-to-all-start.2) | async-done | bytes 4194336 | tf_op jit(solution)/shard_map/all_to_all | solution.py:121
  404.7 7.7 %all-to-all-start.4 = ((bf16[64,256,128]{2,1,0:T(8,128)(2,1)}), bf16[64,256,128]{2,1,0:T(8,128)(2,1)}, u32[]{:S(2)}, u32[]{:S(2)}) async-start(bf16[64,256,128]{2,1,0:T(8,128)(2,1)} %bitcast.181), calls=%async_computation.4 | async-start | bytes 8388608 | tf_op jit(solution)/shard_map/all_to_all | solution.py:121
  412.9 8.5 %fusion.3 = (f32[32,128,128]{1,2,0:T(8,128)}, f32[32,128,128]{1,2,0:T(8,128)}) fusion(f32[32,2,1,128,128]{3,4,1,0,2:T(8,128)} %bitcast.186, f32[32,128,128]{1,2,0:T(8,128)} %get-tuple-element.18, f32[32,2]{1,0:T(8,128)S(1)} %mul.138, pred[32,2,128]{2,1,0:T(4,128)(4,1)S(1)} %get-tuple-element.31, pred[32,2,128]{2,1,0:T(4,128)(4,1)S(1)} %get-tuple-element.32, ...), kind=kLoop, calls=%fused_computation.8 | loop fusion | flops 8388608 | bytes 16794112 | tf_op jit(solution)/shard_map/reduce_sum | solution.py:114
  427.6 5.5 fusion.92
  446.8 60.3 %all-to-all-done.4 = bf16[64,256,128]{2,1,0:T(8,128)(2,1)} async-done(((bf16[64,256,128]{2,1,0:T(8,128)(2,1)}), bf16[64,256,128]{2,1,0:T(8,128)(2,1)}, u32[]{:S(2)}, u32[]{:S(2)}) %all-to-all-start.4) | async-done | bytes 4194336 | tf_op jit(solution)/shard_map/all_to_all | solution.py:121
  507.0 5.5 fusion.95
  525.1 9.3 %all-to-all-start.5 = ((f32[256,2,2,128]{3,2,1,0:T(2,128)}), f32[256,2,2,128]{3,2,1,0:T(2,128)S(1)}, u32[]{:S(2)}, u32[]{:S(2)}) async-start(f32[256,2,2,128]{3,2,1,0:T(2,128)} %copy.167), calls=%async_computation.5 | async-start | bytes 1048576 | tf_op jit(solution)/shard_map/all_to_all | solution.py:145
  535.0 19.3 %all-to-all-done.5 = f32[256,2,2,128]{3,2,1,0:T(2,128)S(1)} async-done(((f32[256,2,2,128]{3,2,1,0:T(2,128)}), f32[256,2,2,128]{3,2,1,0:T(2,128)S(1)}, u32[]{:S(2)}, u32[]{:S(2)}) %all-to-all-start.5) | async-done | bytes 524320 | tf_op jit(solution)/shard_map/all_to_all | solution.py:145
  (88 shorter events, 88.3 us)
Async XLA Ops:
  5.2 38.1 %all-to-all-start = ((s32[64,1,2]{2,1,0:T(1,128)}), s32[64,1,2]{2,1,0:T(1,128)S(1)}, u32[]{:S(2)}, u32[]{:S(2)}) async-start(s32[64,1,2]{2,1,0:T(1,128)} %bitcast.19), calls=%async_computation | async-start | bytes 65536 | tf_op jit(solution)/shard_map/all_to_all | solution.py:65
  19.8 0.7 copy-start.7
  19.8 1.6 copy-start.2
  21.4 0.9 copy-start.3
  21.4 12.1 %copy-start.6 = (s32[32,2]{0,1:T(2,128)S(1)}, s32[32,2]{0,1:T(2,128)}, u32[]{:S(2)}) copy-start(s32[32,2]{0,1:T(2,128)} %param.10) | copy-start | bytes 772
  22.3 11.2 %copy-start = (bf16[32,1,128,128]{3,2,1,0:T(8,128)(2,1)}, bf16[32,1,128,128]{3,2,1,0:T(8,128)(2,1)S(1)}, u32[]{:S(2)}) copy-start(bf16[32,1,128,128]{3,2,1,0:T(8,128)(2,1)S(1)} %get-tuple-element.6) | copy-start | bytes 3145732
  33.5 2.7 copy-start.1
  50.7 107.6 %all-to-all-start.1 = ((bf16[64,256,128]{2,1,0:T(8,128)(2,1)}), bf16[64,256,128]{2,1,0:T(8,128)(2,1)}, u32[]{:S(2)}, u32[]{:S(2)}) async-start(bf16[64,256,128]{2,1,0:T(8,128)(2,1)} %bitcast.183), calls=%async_computation.1 | async-start | bytes 8388608 | tf_op jit(solution)/shard_map/all_to_all | solution.py:103
  158.3 7.6 %copy-start.4 = (s32[32,2,2]{0,2,1:T(2,128)S(1)}, s32[32,2,2]{0,2,1:T(2,128)}, u32[]{:S(2)}) copy-start(s32[32,2,2]{0,2,1:T(2,128)} %param.17) | copy-start | bytes 1540
  158.3 7.8 %copy-start.5 = (s32[32,2,2]{0,2,1:T(2,128)S(1)}, s32[32,2,2]{0,2,1:T(2,128)}, u32[]{:S(2)}) copy-start(s32[32,2,2]{0,2,1:T(2,128)} %param.16) | copy-start | bytes 1540
  158.3 102.3 %all-to-all-start.3 = ((bf16[64,256,128]{2,1,0:T(8,128)(2,1)}), bf16[64,256,128]{2,1,0:T(8,128)(2,1)}, u32[]{:S(2)}, u32[]{:S(2)}) async-start(bf16[64,256,128]{2,1,0:T(8,128)(2,1)} %bitcast.182), calls=%async_computation.3 | async-start | bytes 8388608 | tf_op jit(solution)/shard_map/all_to_all | solution.py:103
  302.5 102.2 %all-to-all-start.2 = ((bf16[64,256,128]{2,1,0:T(8,128)(2,1)}), bf16[64,256,128]{2,1,0:T(8,128)(2,1)}, u32[]{:S(2)}, u32[]{:S(2)}) async-start(bf16[64,256,128]{2,1,0:T(8,128)(2,1)} %bitcast.184), calls=%async_computation.2 | async-start | bytes 8388608 | tf_op jit(solution)/shard_map/all_to_all | solution.py:121
  404.7 102.4 %all-to-all-start.4 = ((bf16[64,256,128]{2,1,0:T(8,128)(2,1)}), bf16[64,256,128]{2,1,0:T(8,128)(2,1)}, u32[]{:S(2)}, u32[]{:S(2)}) async-start(bf16[64,256,128]{2,1,0:T(8,128)(2,1)} %bitcast.181), calls=%async_computation.4 | async-start | bytes 8388608 | tf_op jit(solution)/shard_map/all_to_all | solution.py:121
  525.1 29.1 %all-to-all-start.5 = ((f32[256,2,2,128]{3,2,1,0:T(2,128)}), f32[256,2,2,128]{3,2,1,0:T(2,128)S(1)}, u32[]{:S(2)}, u32[]{:S(2)}) async-start(f32[256,2,2,128]{3,2,1,0:T(2,128)} %copy.167), calls=%async_computation.5 | async-start | bytes 1048576 | tf_op jit(solution)/shard_map/all_to_all | solution.py:145

commit v7 on v6

--- a/solution.py
+++ b/solution.py
@@ -67,6 +67,10 @@
     served_selection = (
         incoming[:, None] - 1 == jnp.arange(exp_dev, dtype=jnp.int32)[None, :]
     ).astype(jnp.bfloat16)
+    serve_index = jnp.clip(incoming - 1, 0, exp_dev - 1)
+    send_index = jnp.zeros((slots_all,), jnp.int32).at[slot].set(
+        jnp.arange(queries, dtype=jnp.int32)
+    )
     owners = (incoming[None, :] - 1 == jnp.arange(exp_dev, dtype=jnp.int32)[:, None]).astype(
         jnp.bfloat16
     )
@@ -96,9 +100,7 @@
         matched = jnp.einsum(
             "evy,edyx->edvx", along_rows, half_done, preferred_element_type=jnp.float32
         ).astype(jnp.bfloat16)
-        served = jnp.einsum(
-            "lm,muqo->luqo", served_selection, matched, preferred_element_type=jnp.float32
-        ).astype(jnp.bfloat16)
+        served = jnp.take(matched, serve_index, axis=0, mode="clip")
         served = served.reshape(n_exp, cap * pixels, pixels)
         returned = lax.all_to_all(served, "exp", split_axis=0, concat_axis=0, tiled=True)
         partners = jnp.einsum(
@@ -114,9 +116,7 @@
         adj_own = jnp.sum(resid, axis=1)
         resid_low = resid.reshape(queries, 1, pixels, pixels).astype(jnp.bfloat16)
         returned_images = apply_shift(resid_low, back_rows, back_cols).astype(jnp.bfloat16)
-        sending_images = jnp.einsum(
-            "ea,ajhv->ejhv", placement_table, returned_images, preferred_element_type=jnp.float32
-        ).astype(jnp.bfloat16)
+        sending_images = jnp.take(returned_images, send_index, axis=0, mode="clip")
         sending_images = sending_images.reshape(n_exp, cap * pixels, pixels)
         arrived = lax.all_to_all(
             sending_images, "exp", split_axis=0, concat_axis=0, tiled=True

time: 565 us -> 561 us (level)
  matrix products: 102 us -> 89.9 us
  local copies, waits for them, and re-layouts: 51.8 us -> 61.8 us
    gather x0 -> x8, local copies, waits for them, and re-layouts: none -> 40.8 us  [the longest x4 22 us: body(): sending_images = jnp.take(returned_images, send_index, axis=0, mode='clip')]
    convert_element_type x4 -> x0, local copies, waits for them, and re-layouts: 18.6 us -> none  [the longest x2 9.31 us: body(): served = jnp.einsum('lm,muqo->luqo', served_selection, matched, preferred...]
    dot_general x4 -> x0, matrix products: 10.9 us -> none  [the longest x2 5.9 us: body(): jnp.einsum('ea,ajhv->ejhv', placement_table, returned_images, preferred_e...]
    another operation x2 -> x0, local copies, waits for them, and re-layouts: 8.3 us -> none
where the time goes in v7:
time: 561 us; the launch traced here: 554 us
  waiting for transfers between devices  320 us (57%)
  matrix products  89.9 us (16%)
  local copies, waits for them, and re-layouts  61.8 us (11%)
  starting transfers between devices  56.8 us (10%)
  other arithmetic  12.3 us (2%)
  blocking collectives  11.2 us (2%)
    all_to_all x2, waiting for transfers between devices, body(): lax.all_to_all(served, 'exp', split_axis=0, concat_axis=0, tiled=True)  164 us
    all_to_all x2, waiting for transfers between devices, body(): lax.all_to_all(sending_images, 'exp', split_axis=0, concat_axis=0, tiled=...  137 us
    dot_general x4, matrix products, apply_shift(): jnp.einsum('qyu,qdux->qdyx', row_mats, partial_cols, preferred_element_ty...  31 us
    gather x4, local copies, waits for them, and re-layouts, body(): sending_images = jnp.take(returned_images, send_index, axis=0, mode='clip')  22 us
    all_to_all x2, starting transfers between devices, body(): lax.all_to_all(served, 'exp', split_axis=0, concat_axis=0, tiled=True)  20.4 us
    all_to_all x1, waiting for transfers between devices, body(): lax.all_to_all(by_block, ('exp', 'det'), split_axis=0, concat_axis=0, til...  19.3 us
    gather x4, local copies, waits for them, and re-layouts, body(): served = jnp.take(matched, serve_index, axis=0, mode='clip')  18.8 us
    all_to_all x2, starting transfers between devices, body(): lax.all_to_all(sending_images, 'exp', split_axis=0, concat_axis=0, tiled=...  14 us
  transfers between devices with their start and end apart: 6, of which 5 were waited for; matrix products, arithmetic and copies ran while one was open for 16% of the time, Pallas kernels for 0%

profile of v7, /device:TPU:1, one launch (start us, length us, event | category | flops | bytes accessed | tf_op | source)
XLA Modules:
  0.0 553.9 jit_solution(12697107505060603698)
XLA Ops:
  5.2 13.1 %all-to-all-start = ((s32[64,1,2]{2,1,0:T(1,128)}), s32[64,1,2]{2,1,0:T(1,128)S(1)}, u32[]{:S(2)}, u32[]{:S(2)}) async-start(s32[64,1,2]{2,1,0:T(1,128)} %bitcast.21), calls=%async_computation | async-start | bytes 65536 | tf_op jit(solution)/shard_map/all_to_all | solution.py:65
  22.6 11.2 %all_gather.3 = f32[8,128,128]{2,1,0:T(8,128)S(1)} all-gather(f32[2,128,128]{2,1,0:T(8,128)S(1)} %copy-done.6), channel_id=1, replica_groups=mesh['exp'=64,'det'=4] {'det'}, dimensions={0}, use_global_device_ids=true | all-gather | bytes 655360 | tf_op jit(solution)/shard_map/all_gather | solution.py:35
  43.9 6.4 %copy.114 = bf16[128,128,128]{2,1,0:T(8,128)(2,1)} copy(bf16[128,128,128]{1,2,0:T(8,128)(2,1)} %gather_fusion) | data formatting | bytes 8388608 | tf_op jit(solution)/shard_map/jit(_take)/gather | solution.py:103
  50.3 13.2 %all-to-all-start.1 = ((bf16[64,256,128]{2,1,0:T(8,128)(2,1)}), bf16[64,256,128]{2,1,0:T(8,128)(2,1)}, u32[]{:S(2)}, u32[]{:S(2)}) async-start(bf16[64,256,128]{2,1,0:T(8,128)(2,1)} %bitcast.177), calls=%async_computation.1 | async-start | bytes 8388608 | tf_op jit(solution)/shard_map/all_to_all | solution.py:105
  74.3 6.3 %copy.136 = bf16[128,128,128]{2,1,0:T(8,128)(2,1)} copy(bf16[128,128,128]{1,2,0:T(8,128)(2,1)} %gather_fusion.2) | data formatting | bytes 8388608 | tf_op jit(solution)/shard_map/jit(_take)/gather | solution.py:103
  80.7 77.4 %all-to-all-done.1 = bf16[64,256,128]{2,1,0:T(8,128)(2,1)} async-done(((bf16[64,256,128]{2,1,0:T(8,128)(2,1)}), bf16[64,256,128]{2,1,0:T(8,128)(2,1)}, u32[]{:S(2)}, u32[]{:S(2)}) %all-to-all-start.1) | async-done | bytes 4194336 | tf_op jit(solution)/shard_map/all_to_all | solution.py:105
  158.1 7.2 %all-to-all-start.3 = ((bf16[64,256,128]{2,1,0:T(8,128)(2,1)}), bf16[64,256,128]{2,1,0:T(8,128)(2,1)}, u32[]{:S(2)}, u32[]{:S(2)}) async-start(bf16[64,256,128]{2,1,0:T(8,128)(2,1)} %bitcast.176), calls=%async_computation.3 | async-start | bytes 8388608 | tf_op jit(solution)/shard_map/all_to_all | solution.py:105
  167.0 6.5 %fusion.86 = bf16[64,128,128]{2,0,1:T(8,128)(2,1)} fusion(bf16[128,128,128]{2,1,0:T(8,128)(2,1)} %bitcast.23, s32[64]{0:T(128)S(1)} %multiply_add_fusion), kind=kOutput, calls=%fused_computation.79 | convolution fusion | flops 269492224 | bytes 6291712 | tf_op jit(solution)/shard_map/fj,fvhm->jvhm/dot_general | solution.py:106
  173.5 86.7 %all-to-all-done.3 = bf16[64,256,128]{2,1,0:T(8,128)(2,1)} async-done(((bf16[64,256,128]{2,1,0:T(8,128)(2,1)}), bf16[64,256,128]{2,1,0:T(8,128)(2,1)}, u32[]{:S(2)}, u32[]{:S(2)}) %all-to-all-start.3) | async-done | bytes 4194336 | tf_op jit(solution)/shard_map/all_to_all | solution.py:105
  260.2 6.5 %fusion.89 = bf16[64,128,128]{2,0,1:T(8,128)(2,1)} fusion(bf16[128,128,128]{2,1,0:T(8,128)(2,1)} %bitcast.52, s32[64]{0:T(128)S(1)} %multiply_add_fusion), kind=kOutput, calls=%fused_computation.80 | convolution fusion | flops 269492224 | bytes 6291712 | tf_op jit(solution)/shard_map/fj,fvhm->jvhm/dot_general | solution.py:106
  266.7 6.9 %fusion.21 = f32[64,128,128]{2,1,0:T(8,128)} fusion(s32[64,128]{1,0:T(8,128)S(1)} %get-tuple-element.29, bf16[64,128,128]{2,0,1:T(8,128)(2,1)} %fusion.86, s32[64,128]{1,0:T(8,128)S(1)} %get-tuple-element.30), kind=kOutput, calls=%fused_computation.36 | convolution fusion | flops 540016640 | bytes 6356992 | tf_op jit(solution)/shard_map/qyu,qdux->qdyx/dot_general | solution.py:18
  273.6 9.7 %fusion.7 = (bf16[64,1,128,128]{2,3,0,1:T(8,128)(2,1)}, bf16[64,1,128,128]{2,3,0,1:T(8,128)(2,1)}, f32[64,128,128]{2,1,0:T(8,128)}) fusion(f32[32,128,128]{1,2,0:T(8,128)} %get-tuple-element.20, f32[64]{0:T(128)S(1)} %get-tuple-element.16, pred[64,128]{1,0:T(8,128)(4,1)S(1)} %get-tuple-element.31, pred[64,128]{1,0:T(8,128)(4,1)S(1)} %get-tuple-element.32, ...), kind=kOutput, calls=%fused_computation.17 | convolution fusion | flops 549453824 | bytes 18956800 | tf_op jit(solution)/shard_map/qyu,qdux->qdyx/dot_general | solution.py:18
  283.2 7.3 %convert_bitcast_fusion.1 = bf16[64,128,128]{1,2,0:T(8,128)(2,1)} fusion(s32[64,128]{1,0:T(8,128)S(1)} %get-tuple-element.35, bf16[64,1,128,128]{2,3,0,1:T(8,128)(2,1)} %get-tuple-element.13, s32[64,128]{1,0:T(8,128)S(1)} %get-tuple-element.36), kind=kOutput, calls=%fused_computation.67 | convolution fusion | flops 541065216 | bytes 4259840 | tf_op jit(solution)/shard_map/qyu,qdux->qdyx/dot_general | solution.py:18
  295.1 6.4 %copy.122 = bf16[128,128,128]{2,1,0:T(8,128)(2,1)} copy(bf16[128,128,128]{1,2,0:T(8,128)(2,1)} %gather_fusion.1) | data formatting | bytes 8388608 | tf_op jit(solution)/shard_map/jit(_take)/gather | solution.py:119
  301.5 7.0 %all-to-all-start.2 = ((bf16[64,256,128]{2,1,0:T(8,128)(2,1)}), bf16[64,256,128]{2,1,0:T(8,128)(2,1)}, u32[]{:S(2)}, u32[]{:S(2)}) async-start(bf16[64,256,128]{2,1,0:T(8,128)(2,1)} %bitcast.178), calls=%async_computation.2 | async-start | bytes 8388608 | tf_op jit(solution)/shard_map/all_to_all | solution.py:121
  308.5 7.2 %convert_bitcast_fusion = bf16[64,128,128]{1,2,0:T(8,128)(2,1)} fusion(s32[64,128]{1,0:T(8,128)S(1)} %get-tuple-element.35, bf16[64,1,128,128]{2,3,0,1:T(8,128)(2,1)} %get-tuple-element.12, s32[64,128]{1,0:T(8,128)S(1)} %get-tuple-element.36), kind=kOutput, calls=%fused_computation.64 | convolution fusion | flops 541065216 | bytes 4259840 | tf_op jit(solution)/shard_map/qyu,qdux->qdyx/dot_general | solution.py:18
  320.4 6.3 %copy.142 = bf16[128,128,128]{2,1,0:T(8,128)(2,1)} copy(bf16[128,128,128]{1,2,0:T(8,128)(2,1)} %gather_fusion.3) | data formatting | bytes 8388608 | tf_op jit(solution)/shard_map/jit(_take)/gather | solution.py:119
  326.8 76.7 %all-to-all-done.2 = bf16[64,256,128]{2,1,0:T(8,128)(2,1)} async-done(((bf16[64,256,128]{2,1,0:T(8,128)(2,1)}), bf16[64,256,128]{2,1,0:T(8,128)(2,1)}, u32[]{:S(2)}, u32[]{:S(2)}) %all-to-all-start.2) | async-done | bytes 4194336 | tf_op jit(solution)/shard_map/all_to_all | solution.py:121
  403.4 7.0 %all-to-all-start.4 = ((bf16[64,256,128]{2,1,0:T(8,128)(2,1)}), bf16[64,256,128]{2,1,0:T(8,128)(2,1)}, u32[]{:S(2)}, u32[]{:S(2)}) async-start(bf16[64,256,128]{2,1,0:T(8,128)(2,1)} %bitcast.175), calls=%async_computation.4 | async-start | bytes 8388608 | tf_op jit(solution)/shard_map/all_to_all | solution.py:121
  411.1 8.5 %fusion.3 = (f32[32,128,128]{1,2,0:T(8,128)}, f32[32,128,128]{1,2,0:T(8,128)}) fusion(f32[32,2,1,128,128]{3,4,1,0,2:T(8,128)} %bitcast.180, f32[32,128,128]{1,2,0:T(8,128)} %get-tuple-element.20, f32[32,2]{1,0:T(8,128)S(1)} %mul.138, pred[32,2,128]{2,1,0:T(4,128)(4,1)S(1)} %get-tuple-element.33, pred[32,2,128]{2,1,0:T(4,128)(4,1)S(1)} %get-tuple-element.34, ...), kind=kLoop, calls=%fused_computation.13 | loop fusion | flops 8388608 | bytes 16794112 | tf_op jit(solution)/shard_map/reduce_sum | solution.py:116
  444.9 60.4 %all-to-all-done.4 = bf16[64,256,128]{2,1,0:T(8,128)(2,1)} async-done(((bf16[64,256,128]{2,1,0:T(8,128)(2,1)}), bf16[64,256,128]{2,1,0:T(8,128)(2,1)}, u32[]{:S(2)}, u32[]{:S(2)}) %all-to-all-start.4) | async-done | bytes 4194336 | tf_op jit(solution)/shard_map/all_to_all | solution.py:121
  505.3 5.5 fusion.95
  523.5 9.3 %all-to-all-start.5 = ((f32[256,2,2,128]{3,2,1,0:T(2,128)}), f32[256,2,2,128]{3,2,1,0:T(2,128)S(1)}, u32[]{:S(2)}, u32[]{:S(2)}) async-start(f32[256,2,2,128]{3,2,1,0:T(2,128)} %copy.151), calls=%async_computation.5 | async-start | bytes 1048576 | tf_op jit(solution)/shard_map/all_to_all | solution.py:145
  533.3 19.3 %all-to-all-done.5 = f32[256,2,2,128]{3,2,1,0:T(2,128)S(1)} async-done(((f32[256,2,2,128]{3,2,1,0:T(2,128)}), f32[256,2,2,128]{3,2,1,0:T(2,128)S(1)}, u32[]{:S(2)}, u32[]{:S(2)}) %all-to-all-start.5) | async-done | bytes 524320 | tf_op jit(solution)/shard_map/all_to_all | solution.py:145
  (95 shorter events, 80.5 us)
Async XLA Ops:
  5.2 35.4 %all-to-all-start = ((s32[64,1,2]{2,1,0:T(1,128)}), s32[64,1,2]{2,1,0:T(1,128)S(1)}, u32[]{:S(2)}, u32[]{:S(2)}) async-start(s32[64,1,2]{2,1,0:T(1,128)} %bitcast.21), calls=%async_computation | async-start | bytes 65536 | tf_op jit(solution)/shard_map/all_to_all | solution.py:65
  19.8 0.7 copy-start.10
  19.8 1.6 copy-start.5
  21.4 1.2 copy-start.6
  21.4 12.4 %copy-start.9 = (s32[32,2]{0,1:T(2,128)S(1)}, s32[32,2]{0,1:T(2,128)}, u32[]{:S(2)}) copy-start(s32[32,2]{0,1:T(2,128)} %param.10) | copy-start | bytes 772
  22.6 13.8 %copy-start.2 = (bf16[32,1,128,128]{3,2,1,0:T(8,128)(2,1)}, bf16[32,1,128,128]{3,2,1,0:T(8,128)(2,1)S(1)}, u32[]{:S(2)}) copy-start(bf16[32,1,128,128]{3,2,1,0:T(8,128)(2,1)S(1)} %get-tuple-element.8) | copy-start | bytes 3145732
  33.8 2.7 copy-start.4
  50.3 13.2 %copy-start = (bf16[32,1,128,128]{3,2,1,0:T(8,128)(2,1)S(1)}, bf16[32,1,128,128]{3,2,1,0:T(8,128)(2,1)}, u32[]{:S(2)}) copy-start(bf16[32,1,128,128]{3,2,1,0:T(8,128)(2,1)} %get-tuple-element.9) | copy-start | bytes 3145732
  50.3 107.7 %all-to-all-start.1 = ((bf16[64,256,128]{2,1,0:T(8,128)(2,1)}), bf16[64,256,128]{2,1,0:T(8,128)(2,1)}, u32[]{:S(2)}, u32[]{:S(2)}) async-start(bf16[64,256,128]{2,1,0:T(8,128)(2,1)} %bitcast.177), calls=%async_computation.1 | async-start | bytes 8388608 | tf_op jit(solution)/shard_map/all_to_all | solution.py:105
  158.1 7.2 %copy-start.7 = (s32[32,2,2]{0,2,1:T(2,128)S(1)}, s32[32,2,2]{0,2,1:T(2,128)}, u32[]{:S(2)}) copy-start(s32[32,2,2]{0,2,1:T(2,128)} %param.17) | copy-start | bytes 1540
  158.1 7.4 %copy-start.8 = (s32[32,2,2]{0,2,1:T(2,128)S(1)}, s32[32,2,2]{0,2,1:T(2,128)}, u32[]{:S(2)}) copy-start(s32[32,2,2]{0,2,1:T(2,128)} %param.16) | copy-start | bytes 1540
  158.1 102.1 %all-to-all-start.3 = ((bf16[64,256,128]{2,1,0:T(8,128)(2,1)}), bf16[64,256,128]{2,1,0:T(8,128)(2,1)}, u32[]{:S(2)}, u32[]{:S(2)}) async-start(bf16[64,256,128]{2,1,0:T(8,128)(2,1)} %bitcast.176), calls=%async_computation.3 | async-start | bytes 8388608 | tf_op jit(solution)/shard_map/all_to_all | solution.py:105
  301.5 101.9 %all-to-all-start.2 = ((bf16[64,256,128]{2,1,0:T(8,128)(2,1)}), bf16[64,256,128]{2,1,0:T(8,128)(2,1)}, u32[]{:S(2)}, u32[]{:S(2)}) async-start(bf16[64,256,128]{2,1,0:T(8,128)(2,1)} %bitcast.178), calls=%async_computation.2 | async-start | bytes 8388608 | tf_op jit(solution)/shard_map/all_to_all | solution.py:121
  403.4 101.9 %all-to-all-start.4 = ((bf16[64,256,128]{2,1,0:T(8,128)(2,1)}), bf16[64,256,128]{2,1,0:T(8,128)(2,1)}, u32[]{:S(2)}, u32[]{:S(2)}) async-start(bf16[64,256,128]{2,1,0:T(8,128)(2,1)} %bitcast.175), calls=%async_computation.4 | async-start | bytes 8388608 | tf_op jit(solution)/shard_map/all_to_all | solution.py:121
  437.7 3.4 copy-start.3
  517.2 2.5 copy-start.1
  523.5 29.1 %all-to-all-start.5 = ((f32[256,2,2,128]{3,2,1,0:T(2,128)}), f32[256,2,2,128]{3,2,1,0:T(2,128)S(1)}, u32[]{:S(2)}, u32[]{:S(2)}) async-start(f32[256,2,2,128]{3,2,1,0:T(2,128)} %copy.151), calls=%async_computation.5 | async-start | bytes 1048576 | tf_op jit(solution)/shard_map/all_to_all | solution.py:145

commit v8 on v7

--- a/solution.py
+++ b/solution.py
@@ -32,8 +32,13 @@
     tap_count = taps.shape[2]
     n_exp = lax.axis_size("exp")
     queries = exp_dev * pair_count
-    all_flat = lax.all_gather(flat, "det", axis=0, tiled=True)
-    det_total = all_flat.shape[0]
+    det_total = flat.shape[0] * lax.axis_size("det")
+    placed = lax.dynamic_update_slice(
+        jnp.zeros((det_total,) + flat.shape[1:], flat.dtype),
+        flat,
+        (lax.axis_index("det") * flat.shape[0], 0, 0),
+    )
+    all_flat = lax.psum(placed, "det")
     pick = (det_ids[:, :, None] == jnp.arange(det_total, dtype=jnp.int32)[None, None, :]).astype(
         jnp.float32
     )

time: 561 us -> 596 us (1.062)
  waiting for transfers between devices: 320 us -> 349 us
  between operations: 1.45 us -> 14.9 us
  blocking collectives: 11.2 us -> 0 us
    psum x0 -> x1, waiting for transfers between devices: none -> 23.6 us  [body(): all_flat = lax.psum(placed, 'det')]
    all_gather x1 -> x0, blocking collectives: 11.2 us -> none  [body(): all_flat = lax.all_gather(flat, 'det', axis=0, tiled=True)]
  transfers between devices with their start and end apart: 6 -> 7, of which waited for: 5 -> 7; matrix products, arithmetic and copies ran while one was open for 16% -> 15% of each run, Pallas kernels for 0% -> 0%
where the time goes in v8:
time: 596 us; the launch traced here: 589 us
  waiting for transfers between devices  349 us (59%)
  matrix products  91.3 us (15%)
  local copies, waits for them, and re-layouts  64.4 us (11%)
  starting transfers between devices  56.7 us (10%)
  between operations  14.9 us (2%)
  other arithmetic  12.3 us (2%)
    all_to_all x2, waiting for transfers between devices, body(): lax.all_to_all(served, 'exp', split_axis=0, concat_axis=0, tiled=True)  164 us
    all_to_all x2, waiting for transfers between devices, body(): lax.all_to_all(sending_images, 'exp', split_axis=0, concat_axis=0, tiled=...  137 us
    dot_general x4, matrix products, apply_shift(): jnp.einsum('qyu,qdux->qdyx', row_mats, partial_cols, preferred_element_ty...  31 us
    psum x1, waiting for transfers between devices, body(): all_flat = lax.psum(placed, 'det')  23.6 us
    gather x4, local copies, waits for them, and re-layouts, body(): sending_images = jnp.take(returned_images, send_index, axis=0, mode='clip')  22 us
    all_to_all x2, starting transfers between devices, body(): lax.all_to_all(served, 'exp', split_axis=0, concat_axis=0, tiled=True)  21.1 us
    all_to_all x1, waiting for transfers between devices, body(): lax.all_to_all(by_block, ('exp', 'det'), split_axis=0, concat_axis=0, til...  19.3 us
    gather x4, local copies, waits for them, and re-layouts, body(): served = jnp.take(matched, serve_index, axis=0, mode='clip')  18.8 us
  transfers between devices with their start and end apart: 7, of which 7 were waited for; matrix products, arithmetic and copies ran while one was open for 15% of the time, Pallas kernels for 0%

profile of v8, /device:TPU:1, one launch (start us, length us, event | category | flops | bytes accessed | tf_op | source)
XLA Modules:
  0.0 588.8 jit_solution(4680663053419937330)
XLA Ops:
  13.7 13.1 %all-to-all-start = ((s32[64,1,2]{2,1,0:T(1,128)}), s32[64,1,2]{2,1,0:T(1,128)S(1)}, u32[]{:S(2)}, u32[]{:S(2)}) async-start(s32[64,1,2]{2,1,0:T(1,128)} %bitcast.21), calls=%async_computation | async-start | bytes 65536 | tf_op jit(solution)/shard_map/all_to_all | solution.py:70
  36.6 23.6 %all-reduce.2.cloned.1.call-done = f32[8,128,128]{2,0,1:T(8,128)} async-done(((f32[8,128,128]{2,0,1:T(8,128)}), f32[8,128,128]{2,0,1:T(8,128)}) %all-reduce.2.cloned.1.call-update) | async-done | bytes 524304 | tf_op jit(solution)/shard_map/psum | solution.py:41
  70.9 6.4 %copy.113 = bf16[128,128,128]{2,1,0:T(8,128)(2,1)} copy(bf16[128,128,128]{1,2,0:T(8,128)(2,1)} %gather_fusion) | data formatting | bytes 8388608 | tf_op jit(solution)/shard_map/jit(_take)/gather | solution.py:108
  77.3 13.9 %all-to-all-start.1 = ((bf16[64,256,128]{2,1,0:T(8,128)(2,1)}), bf16[64,256,128]{2,1,0:T(8,128)(2,1)}, u32[]{:S(2)}, u32[]{:S(2)}) async-start(bf16[64,256,128]{2,1,0:T(8,128)(2,1)} %bitcast.179), calls=%async_computation.1 | async-start | bytes 8388608 | tf_op jit(solution)/shard_map/all_to_all | solution.py:110
  101.9 6.3 %copy.134 = bf16[128,128,128]{2,1,0:T(8,128)(2,1)} copy(bf16[128,128,128]{1,2,0:T(8,128)(2,1)} %gather_fusion.2) | data formatting | bytes 8388608 | tf_op jit(solution)/shard_map/jit(_take)/gather | solution.py:108
  108.3 77.4 %all-to-all-done.1 = bf16[64,256,128]{2,1,0:T(8,128)(2,1)} async-done(((bf16[64,256,128]{2,1,0:T(8,128)(2,1)}), bf16[64,256,128]{2,1,0:T(8,128)(2,1)}, u32[]{:S(2)}, u32[]{:S(2)}) %all-to-all-start.1) | async-done | bytes 4194336 | tf_op jit(solution)/shard_map/all_to_all | solution.py:110
  185.7 7.2 %all-to-all-start.3 = ((bf16[64,256,128]{2,1,0:T(8,128)(2,1)}), bf16[64,256,128]{2,1,0:T(8,128)(2,1)}, u32[]{:S(2)}, u32[]{:S(2)}) async-start(bf16[64,256,128]{2,1,0:T(8,128)(2,1)} %bitcast.178), calls=%async_computation.3 | async-start | bytes 8388608 | tf_op jit(solution)/shard_map/all_to_all | solution.py:110
  194.7 6.5 %fusion.86 = bf16[64,128,128]{2,0,1:T(8,128)(2,1)} fusion(bf16[128,128,128]{2,1,0:T(8,128)(2,1)} %bitcast.23, s32[64]{0:T(128)S(1)} %multiply_add_fusion), kind=kOutput, calls=%fused_computation.79 | convolution fusion | flops 269492224 | bytes 6291712 | tf_op jit(solution)/shard_map/fj,fvhm->jvhm/dot_general | solution.py:111
  201.1 86.7 %all-to-all-done.3 = bf16[64,256,128]{2,1,0:T(8,128)(2,1)} async-done(((bf16[64,256,128]{2,1,0:T(8,128)(2,1)}), bf16[64,256,128]{2,1,0:T(8,128)(2,1)}, u32[]{:S(2)}, u32[]{:S(2)}) %all-to-all-start.3) | async-done | bytes 4194336 | tf_op jit(solution)/shard_map/all_to_all | solution.py:110
  287.8 6.5 %fusion.89 = bf16[64,128,128]{2,0,1:T(8,128)(2,1)} fusion(bf16[128,128,128]{2,1,0:T(8,128)(2,1)} %bitcast.52, s32[64]{0:T(128)S(1)} %multiply_add_fusion), kind=kOutput, calls=%fused_computation.80 | convolution fusion | flops 269492224 | bytes 6291712 | tf_op jit(solution)/shard_map/fj,fvhm->jvhm/dot_general | solution.py:111
  294.3 6.9 %fusion.21 = f32[64,128,128]{2,1,0:T(8,128)} fusion(s32[64,128]{1,0:T(8,128)S(1)} %get-tuple-element.29, bf16[64,128,128]{2,0,1:T(8,128)(2,1)} %fusion.86, s32[64,128]{1,0:T(8,128)S(1)} %get-tuple-element.30), kind=kOutput, calls=%fused_computation.36 | convolution fusion | flops 540016640 | bytes 6356992 | tf_op jit(solution)/shard_map/qyu,qdux->qdyx/dot_general | solution.py:18
  301.2 9.7 %fusion.7 = (bf16[64,1,128,128]{2,3,0,1:T(8,128)(2,1)}, bf16[64,1,128,128]{2,3,0,1:T(8,128)(2,1)}, f32[64,128,128]{2,1,0:T(8,128)}) fusion(f32[32,128,128]{1,2,0:T(8,128)} %get-tuple-element.20, f32[64]{0:T(128)S(1)} %get-tuple-element.16, pred[64,128]{1,0:T(8,128)(4,1)S(1)} %get-tuple-element.31, pred[64,128]{1,0:T(8,128)(4,1)S(1)} %get-tuple-element.32, ...), kind=kOutput, calls=%fused_computation.17 | convolution fusion | flops 549453824 | bytes 18956800 | tf_op jit(solution)/shard_map/qyu,qdux->qdyx/dot_general | solution.py:18
  310.8 7.3 %convert_bitcast_fusion.1 = bf16[64,128,128]{1,2,0:T(8,128)(2,1)} fusion(s32[64,128]{1,0:T(8,128)S(1)} %get-tuple-element.35, bf16[64,1,128,128]{2,3,0,1:T(8,128)(2,1)} %get-tuple-element.13, s32[64,128]{1,0:T(8,128)S(1)} %get-tuple-element.36), kind=kOutput, calls=%fused_computation.67 | convolution fusion | flops 541065216 | bytes 4259840 | tf_op jit(solution)/shard_map/qyu,qdux->qdyx/dot_general | solution.py:18
  322.7 6.4 %copy.121 = bf16[128,128,128]{2,1,0:T(8,128)(2,1)} copy(bf16[128,128,128]{1,2,0:T(8,128)(2,1)} %gather_fusion.1) | data formatting | bytes 8388608 | tf_op jit(solution)/shard_map/jit(_take)/gather | solution.py:124
  329.1 7.0 %all-to-all-start.2 = ((bf16[64,256,128]{2,1,0:T(8,128)(2,1)}), bf16[64,256,128]{2,1,0:T(8,128)(2,1)}, u32[]{:S(2)}, u32[]{:S(2)}) async-start(bf16[64,256,128]{2,1,0:T(8,128)(2,1)} %bitcast.180), calls=%async_computation.2 | async-start | bytes 8388608 | tf_op jit(solution)/shard_map/all_to_all | solution.py:126
  336.1 7.2 %convert_bitcast_fusion = bf16[64,128,128]{1,2,0:T(8,128)(2,1)} fusion(s32[64,128]{1,0:T(8,128)S(1)} %get-tuple-element.35, bf16[64,1,128,128]{2,3,0,1:T(8,128)(2,1)} %get-tuple-element.12, s32[64,128]{1,0:T(8,128)S(1)} %get-tuple-element.36), kind=kOutput, calls=%fused_computation.64 | convolution fusion | flops 541065216 | bytes 4259840 | tf_op jit(solution)/shard_map/qyu,qdux->qdyx/dot_general | solution.py:18
  348.0 6.3 %copy.140 = bf16[128,128,128]{2,1,0:T(8,128)(2,1)} copy(bf16[128,128,128]{1,2,0:T(8,128)(2,1)} %gather_fusion.3) | data formatting | bytes 8388608 | tf_op jit(solution)/shard_map/jit(_take)/gather | solution.py:124
  354.4 76.7 %all-to-all-done.2 = bf16[64,256,128]{2,1,0:T(8,128)(2,1)} async-done(((bf16[64,256,128]{2,1,0:T(8,128)(2,1)}), bf16[64,256,128]{2,1,0:T(8,128)(2,1)}, u32[]{:S(2)}, u32[]{:S(2)}) %all-to-all-start.2) | async-done | bytes 4194336 | tf_op jit(solution)/shard_map/all_to_all | solution.py:126
  431.0 7.0 %all-to-all-start.4 = ((bf16[64,256,128]{2,1,0:T(8,128)(2,1)}), bf16[64,256,128]{2,1,0:T(8,128)(2,1)}, u32[]{:S(2)}, u32[]{:S(2)}) async-start(bf16[64,256,128]{2,1,0:T(8,128)(2,1)} %bitcast.177), calls=%async_computation.4 | async-start | bytes 8388608 | tf_op jit(solution)/shard_map/all_to_all | solution.py:126
  438.7 8.5 %fusion.3 = (f32[32,128,128]{1,2,0:T(8,128)}, f32[32,128,128]{1,2,0:T(8,128)}) fusion(f32[32,2,1,128,128]{3,4,1,0,2:T(8,128)} %bitcast.182, f32[32,128,128]{1,2,0:T(8,128)} %get-tuple-element.20, f32[32,2]{1,0:T(8,128)S(1)} %mul.142, pred[32,2,128]{2,1,0:T(4,128)(4,1)S(1)} %get-tuple-element.33, pred[32,2,128]{2,1,0:T(4,128)(4,1)S(1)} %get-tuple-element.34, ...), kind=kLoop, calls=%fused_computation.13 | loop fusion | flops 8388608 | bytes 16794112 | tf_op jit(solution)/shard_map/reduce_sum | solution.py:121
  453.4 5.5 fusion.92
  472.5 60.4 %all-to-all-done.4 = bf16[64,256,128]{2,1,0:T(8,128)(2,1)} async-done(((bf16[64,256,128]{2,1,0:T(8,128)(2,1)}), bf16[64,256,128]{2,1,0:T(8,128)(2,1)}, u32[]{:S(2)}, u32[]{:S(2)}) %all-to-all-start.4) | async-done | bytes 4194336 | tf_op jit(solution)/shard_map/all_to_all | solution.py:126
  552.4 8.4 %all-to-all-start.5 = ((f32[256,2,2,128]{3,2,1,0:T(2,128)}), f32[256,2,2,128]{3,2,1,0:T(2,128)S(1)}, u32[]{:S(2)}, u32[]{:S(2)}) async-start(f32[256,2,2,128]{3,2,1,0:T(2,128)} %copy.149), calls=%async_computation.5 | async-start | bytes 1048576 | tf_op jit(solution)/shard_map/all_to_all | solution.py:150
  561.4 19.3 %all-to-all-done.5 = f32[256,2,2,128]{3,2,1,0:T(2,128)S(1)} async-done(((f32[256,2,2,128]{3,2,1,0:T(2,128)}), f32[256,2,2,128]{3,2,1,0:T(2,128)S(1)}, u32[]{:S(2)}, u32[]{:S(2)}) %all-to-all-start.5) | async-done | bytes 524320 | tf_op jit(solution)/shard_map/all_to_all | solution.py:150
  (99 shorter events, 89.7 us)
Async XLA Ops:
  7.2 53.0 %all-reduce.2.cloned.1.call-start = ((), (), s32[]{:S(2)}) async-start(), calls=%async_computation.6 | async-start | bytes 1048576 | tf_op jit(solution)/shard_map/psum | solution.py:41
  8.3 0.8 copy-start.6
  13.7 22.6 %all-to-all-start = ((s32[64,1,2]{2,1,0:T(1,128)}), s32[64,1,2]{2,1,0:T(1,128)S(1)}, u32[]{:S(2)}, u32[]{:S(2)}) async-start(s32[64,1,2]{2,1,0:T(1,128)} %bitcast.21), calls=%async_computation | async-start | bytes 65536 | tf_op jit(solution)/shard_map/all_to_all | solution.py:70
  28.3 1.6 copy-start.4
  29.9 1.2 copy-start.9
  29.9 1.2 copy-start.10
  31.1 32.7 %copy-start.2 = (bf16[32,1,128,128]{3,2,1,0:T(8,128)(2,1)}, bf16[32,1,128,128]{3,2,1,0:T(8,128)(2,1)S(1)}, u32[]{:S(2)}) copy-start(bf16[32,1,128,128]{3,2,1,0:T(8,128)(2,1)S(1)} %get-tuple-element.8) | copy-start | bytes 3145732
  77.3 13.9 %copy-start = (bf16[32,1,128,128]{3,2,1,0:T(8,128)(2,1)S(1)}, bf16[32,1,128,128]{3,2,1,0:T(8,128)(2,1)}, u32[]{:S(2)}) copy-start(bf16[32,1,128,128]{3,2,1,0:T(8,128)(2,1)} %get-tuple-element.9) | copy-start | bytes 3145732
  77.3 108.4 %all-to-all-start.1 = ((bf16[64,256,128]{2,1,0:T(8,128)(2,1)}), bf16[64,256,128]{2,1,0:T(8,128)(2,1)}, u32[]{:S(2)}, u32[]{:S(2)}) async-start(bf16[64,256,128]{2,1,0:T(8,128)(2,1)} %bitcast.179), calls=%async_computation.1 | async-start | bytes 8388608 | tf_op jit(solution)/shard_map/all_to_all | solution.py:110
  185.7 7.2 %copy-start.7 = (s32[32,2,2]{0,2,1:T(2,128)S(1)}, s32[32,2,2]{0,2,1:T(2,128)}, u32[]{:S(2)}) copy-start(s32[32,2,2]{0,2,1:T(2,128)} %param.17) | copy-start | bytes 1540
  185.7 7.4 %copy-start.8 = (s32[32,2,2]{0,2,1:T(2,128)S(1)}, s32[32,2,2]{0,2,1:T(2,128)}, u32[]{:S(2)}) copy-start(s32[32,2,2]{0,2,1:T(2,128)} %param.16) | copy-start | bytes 1540
  185.7 102.1 %all-to-all-start.3 = ((bf16[64,256,128]{2,1,0:T(8,128)(2,1)}), bf16[64,256,128]{2,1,0:T(8,128)(2,1)}, u32[]{:S(2)}, u32[]{:S(2)}) async-start(bf16[64,256,128]{2,1,0:T(8,128)(2,1)} %bitcast.178), calls=%async_computation.3 | async-start | bytes 8388608 | tf_op jit(solution)/shard_map/all_to_all | solution.py:110
  329.1 101.9 %all-to-all-start.2 = ((bf16[64,256,128]{2,1,0:T(8,128)(2,1)}), bf16[64,256,128]{2,1,0:T(8,128)(2,1)}, u32[]{:S(2)}, u32[]{:S(2)}) async-start(bf16[64,256,128]{2,1,0:T(8,128)(2,1)} %bitcast.180), calls=%async_computation.2 | async-start | bytes 8388608 | tf_op jit(solution)/shard_map/all_to_all | solution.py:126
  431.0 101.9 %all-to-all-start.4 = ((bf16[64,256,128]{2,1,0:T(8,128)(2,1)}), bf16[64,256,128]{2,1,0:T(8,128)(2,1)}, u32[]{:S(2)}, u32[]{:S(2)}) async-start(bf16[64,256,128]{2,1,0:T(8,128)(2,1)} %bitcast.177), calls=%async_computation.4 | async-start | bytes 8388608 | tf_op jit(solution)/shard_map/all_to_all | solution.py:126
  465.3 3.4 copy-start.3
  544.8 3.2 copy-start.1
  544.8 3.2 copy-start.5
  552.4 28.3 %all-to-all-start.5 = ((f32[256,2,2,128]{3,2,1,0:T(2,128)}), f32[256,2,2,128]{3,2,1,0:T(2,128)S(1)}, u32[]{:S(2)}, u32[]{:S(2)}) async-start(f32[256,2,2,128]{3,2,1,0:T(2,128)} %copy.149), calls=%async_computation.5 | async-start | bytes 1048576 | tf_op jit(solution)/shard_map/all_to_all | solution.py:150
Sparse Core Ops, SparseCore 0:
  10.3 49.8 all-reduce.1
